TPU v7x, 256 devices: a whole 4x4x8 slice. The times are simulated.
256 devices in a mesh: pair: 128 (over x, z, y), aux: 2 (over core).
Axes of the slice: x: 4, y: 4, z: 8, core: 2. Of those that a mesh axis runs over, the one named last changes fastest.
Arguments:
- amplitudes: bfloat16 [16384, 128, 128], P('pair', 'aux'), may hold values from -6 to 6
- k_term: bfloat16 [16384, 128, 128], P('pair', 'aux'), may hold values from -6 to 6
- margin_table: bfloat16 [1024, 128, 128], P('pair'), may hold values from -0.5 to 0.5
- margin_index: int32 [16384], P('pair'), may hold values from 0 to 7
- factors: bfloat16 [128, 512, 128], P('pair', 'aux'), may hold values from -6 to 6
- vir_energy: float32 [16384, 128], P('pair'), may hold values from 0.5 to 3
- occ_energy: float32 [128], replicated, may hold values from -2 to -0.3
- pair_owner: int32 [16384, 1], P('pair'), may hold values from 0 to 127; in each aligned block of 128 rows (0 to 127, 128 to 255, ...) at most 2 rows name the same one
Outputs:
- updated: bfloat16 [16384, 128, 128], P('pair', 'aux')
Inputs may be any that keep to these rules, and one draw needn't show every extreme that they name: `pair_owner`: no more than 2 of the 128 pairs of one aligned block name the same owner. `margin_index`: an index into the 8 margin blocks that belong to the pair's aligned block of 128 pairs.
All inputs are finite; a program needn't handle non-finite values.
Results may differ from a plain program's by a relative error of at most 0.0055.
Values may be sent and summed in bfloat16 or wider, within the bound.
No kernel may reach another device: no remote copies, remote signals or barrier semaphores. Data moves between devices by JAX's collectives and lax.ppermute only.
A program may use at most 128 MiB of HBM per device.

v0:
```python
import jax
import jax.numpy as jnp
from jax import lax
from jax.sharding import PartitionSpec as P


def local(
    amplitudes, k_term, margin_table, margin_index, factors, vir_energy, occ_energy, pair_owner
):
    axis_pairs = lax.axis_size("pair")
    aux_count = lax.axis_size("aux")
    own_index = lax.axis_index("pair")
    aux_index = lax.axis_index("aux")
    pair_count = amplitudes.shape[0]
    row_count = amplitudes.shape[1]
    vir_width = amplitudes.shape[2]
    aux_rows = factors.shape[1]
    ovl_count = margin_table.shape[0]
    capacity = max(2, (2 * pair_count + axis_pairs - 1) // axis_pairs)
    cycle_scale = float(vir_width * aux_rows * aux_count * pair_count) ** (-0.5)
    own_factors = factors[0]
    full_amp = lax.all_gather(amplitudes, "aux", axis=1, tiled=True)
    block_pick = (margin_index[:, None] == jnp.arange(ovl_count, dtype=jnp.int32)[None, :]).astype(
        jnp.bfloat16
    )
    margin = jnp.einsum(
        "po,oab->pab", block_pick, margin_table, preferred_element_type=jnp.float32
    ).astype(jnp.bfloat16)
    halfway = jnp.einsum(
        "pca,pab->pcb", full_amp, margin, preferred_element_type=jnp.float32
    ).astype(jnp.bfloat16)
    rotated = jnp.einsum(
        "pac,pab->pcb", margin, halfway, preferred_element_type=jnp.float32
    ).astype(jnp.bfloat16)
    partial_value = jnp.einsum(
        "pca,qa->pcq", rotated, own_factors, preferred_element_type=jnp.float32
    ).astype(jnp.bfloat16)
    pair_dest = pair_owner[:, 0]
    owner_hits = (pair_dest[:, None] == jnp.arange(axis_pairs, dtype=jnp.int32)[None, :]).astype(
        jnp.int32
    )
    slot_rank = jnp.sum(jnp.cumsum(owner_hits, axis=0) * owner_hits, axis=1) - 1
    slot_index = pair_dest * capacity + slot_rank
    outgoing = (
        jnp.zeros((axis_pairs * capacity, vir_width, aux_rows), jnp.bfloat16)
        .at[slot_index]
        .set(partial_value)
    )
    outgoing = outgoing.reshape(axis_pairs, capacity, vir_width, aux_rows)
    incoming = lax.all_to_all(outgoing, "pair", split_axis=0, concat_axis=0, tiled=True)
    slot_ones = jnp.ones((axis_pairs, capacity), jnp.bfloat16)
    summed = jnp.einsum(
        "sk,skcq->cq", slot_ones, incoming, preferred_element_type=jnp.float32
    ).astype(jnp.bfloat16)
    local_cycle = jnp.dot(summed, own_factors, preferred_element_type=jnp.float32)
    cycle_sum = lax.psum(local_cycle, "aux")
    cycle_vals = (cycle_scale * cycle_sum).astype(jnp.bfloat16)
    cycle_rows = cycle_vals.shape[0]
    slot_back = jnp.broadcast_to(
        cycle_vals[None, None], (axis_pairs, capacity, cycle_rows, vir_width)
    )
    returned = lax.all_to_all(slot_back, "pair", split_axis=0, concat_axis=0, tiled=True)
    own_cycle = returned.reshape(axis_pairs * capacity, cycle_rows, vir_width)[slot_index]
    own_cycle = lax.dynamic_slice_in_dim(own_cycle, aux_index * row_count, row_count, 1)
    cycle_term = jnp.einsum("pca,pba->pcb", own_cycle, margin, preferred_element_type=jnp.float32)
    occ_total = occ_energy.shape[0]
    occ_first = jnp.zeros((pair_count,), jnp.int32) + own_index
    both_ids = jnp.concatenate([occ_first, pair_dest])
    occ_select = (both_ids[:, None] == jnp.arange(occ_total, dtype=jnp.int32)[None, :]).astype(
        jnp.float32
    )
    occ_values = jnp.sum(occ_select * occ_energy[None, :], axis=1)
    occ_sum = occ_values[:pair_count] + occ_values[pair_count:]
    energy_rows = lax.dynamic_slice_in_dim(vir_energy, aux_index * row_count, row_count, 1)
    denominator = energy_rows[:, :, None] + vir_energy[:, None, :] - occ_sum[:, None, None]
    updated = (
        amplitudes.astype(jnp.float32) - (cycle_term + k_term.astype(jnp.float32)) / denominator
    )
    return updated.astype(jnp.bfloat16)


def solution(mesh):
    placed = (
        P("pair", "aux", None),
        P("pair", "aux", None),
        P("pair", None, None),
        P("pair"),
        P("pair", "aux", None),
        P("pair", None),
        P(),
        P("pair", None),
    )
    return jax.shard_map(
        local, mesh=mesh, in_specs=placed, out_specs=P("pair", "aux", None), check_vma=False
    )
```

profile of v0, /device:TPU:32, one launch (start us, length us, event | category | flops | bytes accessed | tf_op | source)
XLA Modules:
  0.0 724.1 jit_solution(5603408930430910391)
XLA Ops:
  6.5 0.7 all-gather.2.cloned.1.call-update
  7.3 0.0 all-reduce.3.cloned.1.call-start
  7.3 0.7 fusion.24
  8.1 0.2 reduce_window_sum.11
  8.2 0.8 select_reduce_fusion.1
  9.1 0.7 fusion.28
  9.7 3.9 convolution_convert_fusion.1
  13.6 17.1 %all-gather.2.cloned.1.call-done = bf16[128,128,128]{2,1,0:T(8,128)(2,1)} async-done(((bf16[128,64,128]{2,1,0:T(8,128)(2,1)}), bf16[128,128,128]{2,1,0:T(8,128)(2,1)}) %all-gather.2.cloned.1.call-update) | async-done | bytes 4194320 | tf_op jit(solution)/shard_map/all_gather | solution.py:22
  30.8 9.4 %fusion.11 = bf16[128,128,128]{2,1,0:T(8,128)(2,1)} fusion(bf16[128,128,128]{2,1,0:T(8,128)(2,1)} %all-gather.2.cloned.1.call-done, bf16[128,128,128]{2,0,1:T(8,128)(2,1)} %convolution_convert_fusion.1), kind=kOutput, calls=%fused_computation.10 | convolution fusion | flops 536870912 | bytes 12582912 | tf_op jit(solution)/shard_map/pca,pab->pcb/dot_general | solution.py:29
  40.2 11.1 %convolution_convert_fusion = bf16[128,128,256]{2,1,0:T(8,128)(2,1)} fusion(bf16[128,128,128]{2,1,0:T(8,128)(2,1)} %fusion.11, bf16[128,128,128]{2,0,1:T(8,128)(2,1)} %convolution_convert_fusion.1, bf16[1,256,128]{2,1,0:T(8,128)(2,1)S(1)} %copy-done.3), kind=kOutput, calls=%fused_computation.4 | convolution fusion | flops 1616904192 | bytes 16842752 | tf_op jit(solution)/shard_map/pca,qa->pcq/dot_general | solution.py:35
  51.2 6.0 broadcast_in_dim.7
  57.2 23.3 %scatter_fusion = bf16[256,128,256]{2,1,0:T(8,128)(2,1)} fusion(bf16[256,128,256]{2,1,0:T(8,128)(2,1)} %broadcast_in_dim.7, s32[128]{0:T(128)S(1)} %fusion.28, bf16[128,128,256]{2,1,0:T(8,128)(2,1)} %convolution_convert_fusion), kind=kCustom, calls=%fused_computation.1 | custom fusion | bytes 25166336 | tf_op jit(solution)/shard_map/scatter | solution.py:47
  80.5 381.0 %all_to_all.10 = bf16[128,2,128,256]{3,2,1,0:T(8,128)(2,1)S(1)} all-to-all(bf16[128,2,128,256]{3,2,1,0:T(8,128)(2,1)} %bitcast.23), channel_id=1, replica_groups=mesh['pair'=128,'aux'=2] {'pair'}, dimensions={0} | all-to-all | bytes 33554432 | tf_op jit(solution)/shard_map/all_to_all | solution.py:50
  461.5 8.9 %fusion = bf16[1,128,256,1]{2,0,3,1:T(2,128)(2,1)S(1)} fusion(bf16[128,2,128,256]{3,2,1,0:T(8,128)(2,1)S(1)} %all_to_all.10), kind=kOutput, calls=%fused_computation.2 | convolution fusion | flops 16777216 | bytes 16842752 | tf_op jit(solution)/shard_map/sk,skcq->cq/dot_general | solution.py:52
  470.4 0.8 fusion.21
  471.2 23.7 %all-reduce.3.cloned.1.call-done = f32[128,128]{1,0:T(8,128)} async-done(((f32[128,128]{1,0:T(8,128)}), f32[128,128]{1,0:T(8,128)}) %all-reduce.3.cloned.1.call-update) | async-done | bytes 65552 | tf_op jit(solution)/shard_map/psum | solution.py:56
  494.9 0.8 multiply_convert_fusion
  495.7 5.3 broadcast_in_dim.8
  501.1 14.3 %all-to-all-start.1 = ((bf16[128,2,128,128]{3,2,1,0:T(8,128)(2,1)}), bf16[128,2,128,128]{3,2,1,0:T(8,128)(2,1)}, u32[]{:S(2)}, u32[]{:S(2)}) async-start(bf16[128,2,128,128]{3,2,1,0:T(8,128)(2,1)} %broadcast_in_dim.8), calls=%async_computation.1 | async-start | bytes 16777216 | tf_op jit(solution)/shard_map/all_to_all | solution.py:62
  515.4 0.1 constant_dynamic-slice_fusion
  515.5 0.2 select_reduce_fusion
  515.7 186.4 %all-to-all-done.1 = bf16[128,2,128,128]{3,2,1,0:T(8,128)(2,1)} async-done(((bf16[128,2,128,128]{3,2,1,0:T(8,128)(2,1)}), bf16[128,2,128,128]{3,2,1,0:T(8,128)(2,1)}, u32[]{:S(2)}, u32[]{:S(2)}) %all-to-all-start.1) | async-done | bytes 8388640 | tf_op jit(solution)/shard_map/all_to_all | solution.py:62
  702.1 6.6 gather_fusion
  708.6 8.6 %subtract_convert_fusion = bf16[128,64,128]{2,1,0:T(8,128)(2,1)} fusion(bf16[128,64,128]{2,1,0:T(8,128)(2,1)} %param.9, bf16[128,64,128]{2,1,0:T(8,128)(2,1)S(1)} %copy-done.2, f32[128]{0:T(128)S(1)} %slice_add_fusion, f32[128,128]{1,0:T(8,128)S(1)} %copy-done.4, f32[128,64]{1,0:T(8,128)S(1)} %constant_dynamic-slice_fusion, ...), kind=kOutput, calls=%fused_computation.5 | convolution fusion | flops 276824064 | bytes 12681732 | tf_op jit(solution)/shard_map/pca,pba->pcb/dot_general | solution.py:65
  (19 shorter events, 0.1 us)
Async XLA Ops:
  6.5 3.2 copy-start
  6.5 24.2 %all-gather.2.cloned.1.call-start = ((), (), s32[]{:S(2)}) async-start(), calls=%async_computation.2 | async-start | bytes 6291456 | tf_op jit(solution)/shard_map/all_gather | solution.py:22
  7.3 487.6 %all-reduce.3.cloned.1.call-start = ((), (), s32[]{:S(2)}) async-start(), calls=%async_computation.3 | async-start | bytes 131072 | tf_op jit(solution)/shard_map/psum | solution.py:56
  13.6 26.5 %copy-start.3 = (bf16[1,256,128]{2,1,0:T(8,128)(2,1)S(1)}, bf16[1,256,128]{2,1,0:T(8,128)(2,1)}, u32[]{:S(2)}) copy-start(bf16[1,256,128]{2,1,0:T(8,128)(2,1)} %param.12) | copy-start | bytes 196612
  501.1 14.3 %copy-start.5 = (s32[128,1]{0,1:T(1,128)S(1)}, s32[128,1]{0,1:T(1,128)}, u32[]{:S(2)}) copy-start(s32[128,1]{0,1:T(1,128)} %param.15) | copy-start | bytes 1540
  501.1 14.3 %copy-start.4 = (f32[128,128]{1,0:T(8,128)S(1)}, f32[128,128]{1,0:T(8,128)}, u32[]{:S(2)}) copy-start(f32[128,128]{1,0:T(8,128)} %param.13) | copy-start | bytes 196612
  501.1 14.4 %copy-start.6 = (f32[128]{0:T(128)S(1)}, f32[128]{0:T(128)}, u32[]{:S(2)}) copy-start(f32[128]{0:T(128)} %param.14) | copy-start | bytes 1540
  501.1 201.0 %all-to-all-start.1 = ((bf16[128,2,128,128]{3,2,1,0:T(8,128)(2,1)}), bf16[128,2,128,128]{3,2,1,0:T(8,128)(2,1)}, u32[]{:S(2)}, u32[]{:S(2)}) async-start(bf16[128,2,128,128]{3,2,1,0:T(8,128)(2,1)} %broadcast_in_dim.8), calls=%async_computation.1 | async-start | bytes 16777216 | tf_op jit(solution)/shard_map/all_to_all | solution.py:62
  702.0 6.6 copy-start.2
  708.6 8.6 %copy-start.1 = (bf16[8,128,128]{2,1,0:T(8,128)(2,1)S(1)}, bf16[8,128,128]{2,1,0:T(8,128)(2,1)}, u32[]{:S(2)}) copy-start(bf16[8,128,128]{2,1,0:T(8,128)(2,1)} %param.10) | copy-start | bytes 786436
Sparse Core Ops, SparseCore 0:
  9.1 21.6 all-gather.1
  471.3 23.5 all-reduce.2
where the time goes:
time: 726 us; the launch traced here: 724 us
  blocking collectives  381 us (52%)
  waiting for transfers between devices  228 us (31%)
  matrix products  42.6 us (6%)
  local copies, waits for them, and re-layouts  41.3 us (6%)
  starting transfers between devices  14.3 us (2%)
  between operations  13.5 us (2%)
    all_to_all x1, blocking collectives, local(): lax.all_to_all(outgoing, 'pair', split_axis=0, concat_axis=0, tiled=True)  381 us
    all_to_all x1, waiting for transfers between devices, local(): lax.all_to_all(slot_back, 'pair', split_axis=0, concat_axis=0, tiled=True)  186 us
    psum x1, waiting for transfers between devices, local(): cycle_sum = lax.psum(local_cycle, 'aux')  23.7 us
    scatter x1, local copies, waits for them, and re-layouts, local(): outgoing = jnp.zeros((axis_pairs * capacity, vir_width, aux_rows), jnp.bf...  23.3 us
    all_gather x1, waiting for transfers between devices, local(): full_amp = lax.all_gather(amplitudes, 'aux', axis=1, tiled=True)  17.1 us
  transfers between devices with their start and end apart: 3, of which 3 were waited for; matrix products, arithmetic and copies ran while one was open for 1% of the time, Pallas kernels for 0%

commit v1 on v0

v1 whole, which is shorter than its diff:
```python
import jax
import jax.numpy as jnp
from jax import lax
from jax.sharding import PartitionSpec as P


def local(
    amplitudes, k_term, margin_table, margin_index, factors, vir_energy, occ_energy, pair_owner
):
    axis_pairs = lax.axis_size("pair")
    aux_count = lax.axis_size("aux")
    own_index = lax.axis_index("pair")
    aux_index = lax.axis_index("aux")
    pair_count = amplitudes.shape[0]
    row_count = amplitudes.shape[1]
    vir_width = amplitudes.shape[2]
    aux_rows = factors.shape[1]
    ovl_count = margin_table.shape[0]
    cycle_scale = float(vir_width * aux_rows * aux_count * pair_count) ** (-0.5)
    every_factor = lax.all_gather(factors[0], ("pair", "aux"), axis=0, tiled=True)
    every_factor = every_factor.reshape(axis_pairs, aux_count * aux_rows, vir_width)
    own_factors = lax.dynamic_index_in_dim(every_factor, own_index, 0, keepdims=False)
    full_amp = lax.all_gather(amplitudes, "aux", axis=1, tiled=True)
    block_pick = (margin_index[:, None] == jnp.arange(ovl_count, dtype=jnp.int32)[None, :]).astype(
        jnp.bfloat16
    )
    margin = jnp.einsum(
        "po,oab->pab", block_pick, margin_table, preferred_element_type=jnp.float32
    ).astype(jnp.bfloat16)
    halfway = jnp.einsum(
        "pca,pab->pcb", full_amp, margin, preferred_element_type=jnp.float32
    ).astype(jnp.bfloat16)
    rotated = jnp.einsum(
        "pac,pab->pcb", margin, halfway, preferred_element_type=jnp.float32
    ).astype(jnp.bfloat16)
    rotated = lax.dynamic_slice_in_dim(rotated, aux_index * row_count, row_count, 1)
    pair_dest = pair_owner[:, 0]
    owner_pick = (
        jnp.arange(axis_pairs, dtype=jnp.int32)[:, None] == pair_dest[None, :]
    ).astype(jnp.bfloat16)
    outgoing = jnp.einsum(
        "jp,pcb->jcb", owner_pick, rotated, preferred_element_type=jnp.float32
    ).astype(jnp.bfloat16)
    incoming = lax.all_to_all(outgoing, "pair", 0, 0, tiled=True)
    dressed = jnp.einsum(
        "ica,iqa->cq", incoming, every_factor, preferred_element_type=jnp.float32
    ).astype(jnp.bfloat16)
    local_cycle = jnp.dot(dressed, own_factors, preferred_element_type=jnp.float32)
    cycle_vals = (cycle_scale * local_cycle).astype(jnp.bfloat16)
    slot_back = jnp.broadcast_to(cycle_vals[None], (axis_pairs, row_count, vir_width))
    returned = lax.all_to_all(slot_back, "pair", 0, 0, tiled=True)
    own_cycle = jnp.einsum(
        "jp,jca->pca", owner_pick, returned, preferred_element_type=jnp.float32
    ).astype(jnp.bfloat16)
    cycle_term = jnp.einsum("pca,pba->pcb", own_cycle, margin, preferred_element_type=jnp.float32)
    occ_sum = occ_energy[own_index] + occ_energy[pair_dest]
    energy_rows = lax.dynamic_slice_in_dim(vir_energy, aux_index * row_count, row_count, 1)
    denominator = energy_rows[:, :, None] + vir_energy[:, None, :] - occ_sum[:, None, None]
    updated = (
        amplitudes.astype(jnp.float32) - (cycle_term + k_term.astype(jnp.float32)) / denominator
    )
    return updated.astype(jnp.bfloat16)


def solution(mesh):
    placed = (
        P("pair", "aux", None),
        P("pair", "aux", None),
        P("pair", None, None),
        P("pair"),
        P("pair", "aux", None),
        P("pair", None),
        P(),
        P("pair", None),
    )
    return jax.shard_map(
        local, mesh=mesh, in_specs=placed, out_specs=P("pair", "aux", None), check_vma=False
    )
```

time: 726 us -> 267 us (0.37)
  blocking collectives: 381 us -> 0 us
  waiting for transfers between devices: 228 us -> 174 us
  local copies, waits for them, and re-layouts: 41.3 us -> 8.68 us
  starting transfers between devices: 14.3 us -> 23.5 us
    all_to_all x1 -> x0, blocking collectives: 381 us -> none  [local(): lax.all_to_all(outgoing, 'pair', split_axis=0, concat_axis=0, tiled=True)]
    all_to_all x1 -> x2, waiting for transfers between devices: 186 us -> 110 us  [the longest x1 59.4 us: local(): incoming = lax.all_to_all(outgoing, 'pair', 0, 0, tiled=True)]
    all_gather x0 -> x1, waiting for transfers between devices: none -> 43.7 us  [local(): lax.all_gather(factors[0], ('pair', 'aux'), axis=0, tiled=True)]
    psum x1 -> x0, waiting for transfers between devices: 23.7 us -> none  [local(): cycle_sum = lax.psum(local_cycle, 'aux')]
    scatter x1 -> x0, local copies, waits for them, and re-layouts: 23.3 us -> none  [local(): outgoing = jnp.zeros((axis_pairs * capacity, vir_width, aux_rows), jnp.bf...]
    broadcast_in_dim x2 -> x1, local copies, waits for them, and re-layouts: 11.3 us -> 1.84 us  [local(): jnp.broadcast_to(cycle_vals[None], (axis_pairs, row_count, vir_width))]
    all_to_all x1 -> x2, starting transfers between devices: 14.3 us -> 23.4 us  [the longest x1 13.7 us: local(): incoming = lax.all_to_all(outgoing, 'pair', 0, 0, tiled=True)]
  transfers between devices with their start and end apart: 3 -> 4, of which waited for: 3 -> 4; matrix products, arithmetic and copies ran while one was open for 1% -> 10% of each run, Pallas kernels for 0% -> 0%
where the time goes in v1:
time: 267 us
  waiting for transfers between devices  174 us (65%)
  matrix products  47.2 us (18%)
  starting transfers between devices  23.5 us (9%)
  between operations  13.5 us (5%)
  local copies, waits for them, and re-layouts  8.68 us (3%)
    all_to_all x1, waiting for transfers between devices, local(): incoming = lax.all_to_all(outgoing, 'pair', 0, 0, tiled=True)  59.4 us
    all_to_all x1, waiting for transfers between devices, local(): returned = lax.all_to_all(slot_back, 'pair', 0, 0, tiled=True)  50.2 us
    all_gather x1, waiting for transfers between devices, local(): lax.all_gather(factors[0], ('pair', 'aux'), axis=0, tiled=True)  43.7 us
    all_gather x1, waiting for transfers between devices, local(): full_amp = lax.all_gather(amplitudes, 'aux', axis=1, tiled=True)  18.9 us
    dot_general x1, matrix products, local(): jnp.einsum('pca,pba->pcb', own_cycle, margin, preferred_element_type=jnp....  15.8 us
    all_to_all x1, starting transfers between devices, local(): incoming = lax.all_to_all(outgoing, 'pair', 0, 0, tiled=True)  13.7 us
    dot_general x1, matrix products, local(): jnp.einsum('pac,pab->pcb', margin, halfway, preferred_element_type=jnp.fl...  13 us
    dot_general x1, matrix products, local(): jnp.dot(dressed, own_factors, preferred_element_type=jnp.float32)  11 us
  transfers between devices with their start and end apart: 4, of which 4 were waited for; matrix products, arithmetic and copies ran while one was open for 10% of the time, Pallas kernels for 0%

profile of v1, /device:TPU:32, one launch (start us, length us, event | category | flops | bytes accessed | tf_op | source)
XLA Modules:
  0.0 267.1 jit_solution(3907826029855658009)
XLA Ops:
  6.5 0.7 all-gather.4.cloned.1.call-update
  7.3 0.0 all-gather.6.cloned.1.call-start
  7.3 0.7 all-gather.6.cloned.1.call-update
  8.0 3.9 %convolution_convert_fusion = bf16[128,128,128]{2,0,1:T(8,128)(2,1)} fusion(bf16[8,128,128]{2,1,0:T(8,128)(2,1)S(1)} %copy-done, s32[128]{0:T(128)} %param.11), kind=kOutput, calls=%fused_computation.11 | convolution fusion | flops 35652608 | bytes 4456960 | tf_op jit(solution)/shard_map/po,oab->pab/dot_general | solution.py:27
  11.9 18.9 %all-gather.4.cloned.1.call-done = bf16[128,128,128]{2,1,0:T(8,128)(2,1)} async-done(((bf16[128,64,128]{2,1,0:T(8,128)(2,1)}), bf16[128,128,128]{2,1,0:T(8,128)(2,1)}) %all-gather.4.cloned.1.call-update) | async-done | bytes 4194320 | tf_op jit(solution)/shard_map/all_gather | solution.py:23
  30.8 13.0 %fusion = bf16[128,128,128]{2,1,0:T(8,128)(2,1)} fusion(bf16[128,128,128]{2,1,0:T(8,128)(2,1)} %all-gather.4.cloned.1.call-done, bf16[128,128,128]{2,0,1:T(8,128)(2,1)} %convolution_convert_fusion), kind=kOutput, calls=%fused_computation.5 | convolution fusion | flops 1075838976 | bytes 12582912 | tf_op jit(solution)/shard_map/pac,pab->pcb/dot_general | solution.py:33
  43.8 1.8 dynamic-slice_convert_fusion
  45.6 1.8 fusion.10
  47.4 2.7 %copy.36 = bf16[128,64,128]{2,1,0:T(8,128)(2,1)} copy(bf16[128,64,128]{2,0,1:T(8,128)(2,1)S(1)} %fusion.10) | data formatting | bytes 4194304 | tf_op jit(solution)/shard_map/jp,pcb->jcb/dot_general | solution.py:41
  50.0 13.7 %all-to-all-start = ((bf16[128,64,128]{2,1,0:T(8,128)(2,1)}), bf16[128,64,128]{2,1,0:T(8,128)(2,1)S(1)}, u32[]{:S(2)}, u32[]{:S(2)}) async-start(bf16[128,64,128]{2,1,0:T(8,128)(2,1)} %copy.36), calls=%async_computation | async-start | bytes 4194304 | tf_op jit(solution)/shard_map/all_to_all | solution.py:44
  63.7 59.4 %all-to-all-done = bf16[128,64,128]{2,1,0:T(8,128)(2,1)S(1)} async-done(((bf16[128,64,128]{2,1,0:T(8,128)(2,1)}), bf16[128,64,128]{2,1,0:T(8,128)(2,1)S(1)}, u32[]{:S(2)}, u32[]{:S(2)}) %all-to-all-start) | async-done | bytes 2097184 | tf_op jit(solution)/shard_map/all_to_all | solution.py:44
  123.1 43.7 %all-gather.6.cloned.1.call-done = bf16[1,65536,128]{2,1,0:T(8,128)(2,1)} async-done(((bf16[1,256,128]{2,1,0:T(8,128)(2,1)}), bf16[1,65536,128]{2,1,0:T(8,128)(2,1)}) %all-gather.6.cloned.1.call-update) | async-done | bytes 16777232 | tf_op jit(solution)/shard_map/all_gather | solution.py:20
  166.8 11.0 %fusion.15 = bf16[64,128]{1,0:T(8,128)(2,1)S(1)} fusion(bf16[128,64,128]{2,1,0:T(8,128)(2,1)S(1)} %all-to-all-done, bf16[128,512,128]{2,1,0:T(8,128)(2,1)} %bitcast.24, s32[]{:T(128)S(6)} %select_n.14), kind=kOutput, calls=%fused_computation.19 | convolution fusion | flops 1082179584 | bytes 19021828 | tf_op jit(solution)/shard_map/dot_general | solution.py:48
  177.9 0.0 copy-start.3
  177.9 1.8 broadcast_in_dim.2
  179.7 9.7 %all-to-all-start.1 = ((bf16[128,64,128]{2,1,0:T(8,128)(2,1)}), bf16[128,64,128]{2,1,0:T(8,128)(2,1)S(1)}, u32[]{:S(2)}, u32[]{:S(2)}) async-start(bf16[128,64,128]{2,1,0:T(8,128)(2,1)} %broadcast_in_dim.2), calls=%async_computation.1 | async-start | bytes 4194304 | tf_op jit(solution)/shard_map/all_to_all | solution.py:51
  189.5 0.6 dynamic_slice.16
  190.1 1.2 gather_fusion
  191.3 0.1 constant_dynamic-slice_fusion
  191.4 0.6 broadcast_add_fusion
  192.1 50.2 %all-to-all-done.1 = bf16[128,64,128]{2,1,0:T(8,128)(2,1)S(1)} async-done(((bf16[128,64,128]{2,1,0:T(8,128)(2,1)}), bf16[128,64,128]{2,1,0:T(8,128)(2,1)S(1)}, u32[]{:S(2)}, u32[]{:S(2)}) %all-to-all-start.1) | async-done | bytes 2097184 | tf_op jit(solution)/shard_map/all_to_all | solution.py:51
  242.3 1.8 fusion.8
  244.0 0.4 copy-done.2
  244.5 15.8 %subtract_convert_fusion = bf16[128,64,128]{2,1,0:T(8,128)(2,1)} fusion(bf16[128,64,128]{2,1,0:T(8,128)(2,1)} %param.9, bf16[128,64,128]{2,1,0:T(8,128)(2,1)} %param.8, f32[128]{0:T(128)S(1)} %broadcast_add_fusion, f32[128,128]{1,0:T(8,128)S(1)} %copy-done.3, f32[128,64]{1,0:T(8,128)S(1)} %constant_dynamic-slice_fusion, ...), kind=kOutput, calls=%fused_computation.4 | convolution fusion | flops 276824064 | bytes 12681728 | tf_op jit(solution)/shard_map/pca,pba->pcb/dot_general | solution.py:55
  (11 shorter events, 0.0 us)
Async XLA Ops:
  6.5 1.5 copy-start
  6.5 24.2 %all-gather.4.cloned.1.call-start = ((), (), s32[]{:S(2)}) async-start(), calls=%async_computation.2 | async-start | bytes 6291456 | tf_op jit(solution)/shard_map/all_gather | solution.py:23
  7.3 159.6 %all-gather.6.cloned.1.call-start = ((), (), s32[]{:S(2)}) async-start(), calls=%async_computation.3 | async-start | bytes 16842752 | tf_op jit(solution)/shard_map/all_gather | solution.py:20
  43.8 1.8 copy-start.4
  50.0 73.1 %all-to-all-start = ((bf16[128,64,128]{2,1,0:T(8,128)(2,1)}), bf16[128,64,128]{2,1,0:T(8,128)(2,1)S(1)}, u32[]{:S(2)}, u32[]{:S(2)}) async-start(bf16[128,64,128]{2,1,0:T(8,128)(2,1)} %copy.36), calls=%async_computation | async-start | bytes 4194304 | tf_op jit(solution)/shard_map/all_to_all | solution.py:44
  177.8 11.6 %copy-start.1 = (f32[128]{0:T(128)S(1)}, f32[128]{0:T(128)}, u32[]{:S(2)}) copy-start(f32[128]{0:T(128)} %param.14) | copy-start | bytes 1540
  177.9 13.5 %copy-start.3 = (f32[128,128]{1,0:T(8,128)S(1)}, f32[128,128]{1,0:T(8,128)}, u32[]{:S(2)}) copy-start(f32[128,128]{1,0:T(8,128)} %param.13) | copy-start | bytes 196612
  179.7 62.6 %all-to-all-start.1 = ((bf16[128,64,128]{2,1,0:T(8,128)(2,1)}), bf16[128,64,128]{2,1,0:T(8,128)(2,1)S(1)}, u32[]{:S(2)}, u32[]{:S(2)}) async-start(bf16[128,64,128]{2,1,0:T(8,128)(2,1)} %broadcast_in_dim.2), calls=%async_computation.1 | async-start | bytes 4194304 | tf_op jit(solution)/shard_map/all_to_all | solution.py:51
  242.3 2.2 copy-start.2
Sparse Core Ops, SparseCore 0:
  9.1 21.6 all-gather.3
  34.5 132.2 all-gather.5

commit v2 on v1

--- a/solution.py
+++ b/solution.py
@@ -20,7 +20,12 @@
     every_factor = lax.all_gather(factors[0], ("pair", "aux"), axis=0, tiled=True)
     every_factor = every_factor.reshape(axis_pairs, aux_count * aux_rows, vir_width)
     own_factors = lax.dynamic_index_in_dim(every_factor, own_index, 0, keepdims=False)
-    full_amp = lax.all_gather(amplitudes, "aux", axis=1, tiled=True)
+    other_amp = lax.ppermute(amplitudes, "aux", perm=[(0, 1), (1, 0)])
+    full_amp = jnp.where(
+        aux_index == 0,
+        jnp.concatenate([amplitudes, other_amp], axis=1),
+        jnp.concatenate([other_amp, amplitudes], axis=1),
+    )
     block_pick = (margin_index[:, None] == jnp.arange(ovl_count, dtype=jnp.int32)[None, :]).astype(
         jnp.bfloat16
     )

time: 267 us -> 245 us (0.918)
  waiting for transfers between devices: 174 us -> 149 us
    all_gather x1 -> x0, waiting for transfers between devices: 18.9 us -> none  [local(): full_amp = lax.all_gather(amplitudes, 'aux', axis=1, tiled=True)]
    all_gather x1, waiting for transfers between devices: 43.7 us -> 38.4 us  [local(): lax.all_gather(factors[0], ('pair', 'aux'), axis=0, tiled=True)]
  transfers between devices with their start and end apart: 4 -> 4, of which waited for: 4 -> 4; matrix products, arithmetic and copies ran while one was open for 10% -> 11% of each run, Pallas kernels for 0% -> 0%
where the time goes in v2:
time: 245 us
  waiting for transfers between devices  149 us (61%)
  matrix products  47.9 us (20%)
  starting transfers between devices  24.9 us (10%)
  between operations  13.5 us (6%)
  local copies, waits for them, and re-layouts  8.79 us (4%)
    all_to_all x1, waiting for transfers between devices, local(): incoming = lax.all_to_all(outgoing, 'pair', 0, 0, tiled=True)  59.4 us
    all_to_all x1, waiting for transfers between devices, local(): returned = lax.all_to_all(slot_back, 'pair', 0, 0, tiled=True)  50.3 us
    all_gather x1, waiting for transfers between devices, local(): lax.all_gather(factors[0], ('pair', 'aux'), axis=0, tiled=True)  38.4 us
    dot_general x1, matrix products, local(): jnp.einsum('pca,pba->pcb', own_cycle, margin, preferred_element_type=jnp....  15.8 us
    all_to_all x1, starting transfers between devices, local(): incoming = lax.all_to_all(outgoing, 'pair', 0, 0, tiled=True)  15 us
    dot_general x1, matrix products, local(): jnp.einsum('pac,pab->pcb', margin, halfway, preferred_element_type=jnp.fl...  13.7 us
    dot_general x1, matrix products, local(): jnp.dot(dressed, own_factors, preferred_element_type=jnp.float32)  11 us
    all_to_all x1, starting transfers between devices, local(): returned = lax.all_to_all(slot_back, 'pair', 0, 0, tiled=True)  9.74 us
  transfers between devices with their start and end apart: 4, of which 4 were waited for; matrix products, arithmetic and copies ran while one was open for 11% of the time, Pallas kernels for 0%

profile of v2, /device:TPU:32, one launch (start us, length us, event | category | flops | bytes accessed | tf_op | source)
XLA Modules:
  0.0 244.9 jit_solution(12907269622363270293)
XLA Ops:
  6.5 0.7 all-gather.3.cloned.1.call-update
  7.3 0.1 collective-permute-start
  7.4 0.1 copy-done
  7.5 3.9 %convolution_convert_fusion = bf16[128,128,128]{2,0,1:T(8,128)(2,1)} fusion(bf16[8,128,128]{2,1,0:T(8,128)(2,1)S(1)} %copy-done, s32[128]{0:T(128)} %param.11), kind=kOutput, calls=%fused_computation.19 | convolution fusion | flops 35652608 | bytes 4456960 | tf_op jit(solution)/shard_map/po,oab->pab/dot_general | solution.py:32
  11.4 0.5 collective-permute-done
  11.9 13.7 %fusion.6 = bf16[128,128,128]{2,1,0:T(8,128)(2,1)} fusion(bf16[128,128,128]{2,0,1:T(8,128)(2,1)} %convolution_convert_fusion, bf16[128,64,128]{2,1,0:T(8,128)(2,1)} %collective-permute-done, bf16[128,64,128]{2,1,0:T(8,128)(2,1)S(1)} %copy-done.5, pred[]{:T(512)S(6)} %eq.38), kind=kOutput, calls=%fused_computation.12 | convolution fusion | flops 1094713344 | bytes 12582913 | tf_op jit(solution)/shard_map/pac,pab->pcb/dot_general | solution.py:38
  25.5 1.8 dynamic-slice_convert_fusion
  27.4 1.8 fusion.19
  29.1 2.7 %copy.41 = bf16[128,64,128]{2,1,0:T(8,128)(2,1)} copy(bf16[128,64,128]{2,0,1:T(8,128)(2,1)S(1)} %fusion.19) | data formatting | bytes 4194304 | tf_op jit(solution)/shard_map/jp,pcb->jcb/dot_general | solution.py:46
  31.8 15.0 %all-to-all-start = ((bf16[128,64,128]{2,1,0:T(8,128)(2,1)}), bf16[128,64,128]{2,1,0:T(8,128)(2,1)S(1)}, u32[]{:S(2)}, u32[]{:S(2)}) async-start(bf16[128,64,128]{2,1,0:T(8,128)(2,1)} %copy.41), calls=%async_computation | async-start | bytes 4194304 | tf_op jit(solution)/shard_map/all_to_all | solution.py:49
  46.8 59.4 %all-to-all-done = bf16[128,64,128]{2,1,0:T(8,128)(2,1)S(1)} async-done(((bf16[128,64,128]{2,1,0:T(8,128)(2,1)}), bf16[128,64,128]{2,1,0:T(8,128)(2,1)S(1)}, u32[]{:S(2)}, u32[]{:S(2)}) %all-to-all-start) | async-done | bytes 2097184 | tf_op jit(solution)/shard_map/all_to_all | solution.py:49
  106.2 38.4 %all-gather.3.cloned.1.call-done = bf16[1,65536,128]{2,1,0:T(8,128)(2,1)} async-done(((bf16[1,256,128]{2,1,0:T(8,128)(2,1)}), bf16[1,65536,128]{2,1,0:T(8,128)(2,1)}) %all-gather.3.cloned.1.call-update) | async-done | bytes 16777232 | tf_op jit(solution)/shard_map/all_gather | solution.py:20
  144.7 11.0 %fusion.24 = bf16[64,128]{1,0:T(8,128)(2,1)S(1)} fusion(bf16[128,64,128]{2,1,0:T(8,128)(2,1)S(1)} %all-to-all-done, bf16[128,512,128]{2,1,0:T(8,128)(2,1)} %bitcast.23, s32[]{:T(128)S(6)} %select_n.24), kind=kOutput, calls=%fused_computation.27 | convolution fusion | flops 1082179584 | bytes 19021828 | tf_op jit(solution)/shard_map/dot_general | solution.py:53
  155.7 0.0 copy-start.3
  155.7 1.8 broadcast_in_dim.2
  157.5 9.7 %all-to-all-start.1 = ((bf16[128,64,128]{2,1,0:T(8,128)(2,1)}), bf16[128,64,128]{2,1,0:T(8,128)(2,1)S(1)}, u32[]{:S(2)}, u32[]{:S(2)}) async-start(bf16[128,64,128]{2,1,0:T(8,128)(2,1)} %broadcast_in_dim.2), calls=%async_computation.1 | async-start | bytes 4194304 | tf_op jit(solution)/shard_map/all_to_all | solution.py:56
  167.3 0.6 dynamic_slice.16
  167.9 1.2 gather_fusion
  169.1 0.1 constant_dynamic-slice_fusion
  169.2 0.6 broadcast_add_fusion
  169.8 50.3 %all-to-all-done.1 = bf16[128,64,128]{2,1,0:T(8,128)(2,1)S(1)} async-done(((bf16[128,64,128]{2,1,0:T(8,128)(2,1)}), bf16[128,64,128]{2,1,0:T(8,128)(2,1)S(1)}, u32[]{:S(2)}, u32[]{:S(2)}) %all-to-all-start.1) | async-done | bytes 2097184 | tf_op jit(solution)/shard_map/all_to_all | solution.py:56
  220.1 1.8 fusion.17
  221.9 0.4 copy-done.2
  222.3 15.8 %subtract_convert_fusion = bf16[128,64,128]{2,1,0:T(8,128)(2,1)} fusion(bf16[128,64,128]{2,1,0:T(8,128)(2,1)} %param.9, bf16[128,64,128]{2,1,0:T(8,128)(2,1)} %param.8, f32[128]{0:T(128)S(1)} %broadcast_add_fusion, f32[128,128]{1,0:T(8,128)S(1)} %copy-done.3, f32[128,64]{1,0:T(8,128)S(1)} %constant_dynamic-slice_fusion, ...), kind=kOutput, calls=%fused_computation.11 | convolution fusion | flops 276824064 | bytes 12681728 | tf_op jit(solution)/shard_map/pca,pba->pcb/dot_general | solution.py:60
  (12 shorter events, 0.0 us)
Async XLA Ops:
  6.5 1.0 copy-start
  6.5 5.3 %copy-start.5 = (bf16[128,64,128]{2,1,0:T(8,128)(2,1)S(1)}, bf16[128,64,128]{2,1,0:T(8,128)(2,1)}, u32[]{:S(2)}) copy-start(bf16[128,64,128]{2,1,0:T(8,128)(2,1)} %param.8) | copy-start | bytes 6291460
  6.5 138.1 %all-gather.3.cloned.1.call-start = ((), (), s32[]{:S(2)}) async-start(), calls=%async_computation.2 | async-start | bytes 16842752 | tf_op jit(solution)/shard_map/all_gather | solution.py:20
  7.3 4.6 %collective-permute-start = (bf16[128,64,128]{2,1,0:T(8,128)(2,1)}, bf16[128,64,128]{2,1,0:T(8,128)(2,1)}, u32[]{:S(2)}, u32[]{:S(2)}) collective-permute-start(bf16[128,64,128]{2,1,0:T(8,128)(2,1)} %param.8), channel_id=1, source_target_pairs={{0,1},{1,0},{2,3},{3,2},{4,5},{5,4},{6,7},{7,6},{8,9},{9,8},{10,11... | collective-permute-start | bytes 6291464 | tf_op jit(solution)/shard_map/ppermute | solution.py:23
  25.5 1.8 copy-start.4
  31.8 74.4 %all-to-all-start = ((bf16[128,64,128]{2,1,0:T(8,128)(2,1)}), bf16[128,64,128]{2,1,0:T(8,128)(2,1)S(1)}, u32[]{:S(2)}, u32[]{:S(2)}) async-start(bf16[128,64,128]{2,1,0:T(8,128)(2,1)} %copy.41), calls=%async_computation | async-start | bytes 4194304 | tf_op jit(solution)/shard_map/all_to_all | solution.py:49
  155.7 11.6 %copy-start.1 = (f32[128]{0:T(128)S(1)}, f32[128]{0:T(128)}, u32[]{:S(2)}) copy-start(f32[128]{0:T(128)} %param.14) | copy-start | bytes 1540
  155.7 13.5 %copy-start.3 = (f32[128,128]{1,0:T(8,128)S(1)}, f32[128,128]{1,0:T(8,128)}, u32[]{:S(2)}) copy-start(f32[128,128]{1,0:T(8,128)} %param.13) | copy-start | bytes 196612
  157.5 62.6 %all-to-all-start.1 = ((bf16[128,64,128]{2,1,0:T(8,128)(2,1)}), bf16[128,64,128]{2,1,0:T(8,128)(2,1)S(1)}, u32[]{:S(2)}, u32[]{:S(2)}) async-start(bf16[128,64,128]{2,1,0:T(8,128)(2,1)} %broadcast_in_dim.2), calls=%async_computation.1 | async-start | bytes 4194304 | tf_op jit(solution)/shard_map/all_to_all | solution.py:56
  220.1 2.2 copy-start.2
Sparse Core Ops, SparseCore 0:
  11.0 133.5 all-gather.2

commit v3 on v2

--- a/solution.py
+++ b/solution.py
@@ -46,6 +46,12 @@
     outgoing = jnp.einsum(
         "jp,pcb->jcb", owner_pick, rotated, preferred_element_type=jnp.float32
     ).astype(jnp.bfloat16)
+    occ_sum = occ_energy[own_index] + occ_energy[pair_dest]
+    energy_rows = lax.dynamic_slice_in_dim(vir_energy, aux_index * row_count, row_count, 1)
+    denominator = energy_rows[:, :, None] + vir_energy[:, None, :] - occ_sum[:, None, None]
+    inverse = 1.0 / denominator
+    prior = amplitudes.astype(jnp.float32) - k_term.astype(jnp.float32) * inverse
+    outgoing, prior, inverse = lax.optimization_barrier((outgoing, prior, inverse))
     incoming = lax.all_to_all(outgoing, "pair", 0, 0, tiled=True)
     dressed = jnp.einsum(
         "ica,iqa->cq", incoming, every_factor, preferred_element_type=jnp.float32
@@ -58,12 +64,7 @@
         "jp,jca->pca", owner_pick, returned, preferred_element_type=jnp.float32
     ).astype(jnp.bfloat16)
     cycle_term = jnp.einsum("pca,pba->pcb", own_cycle, margin, preferred_element_type=jnp.float32)
-    occ_sum = occ_energy[own_index] + occ_energy[pair_dest]
-    energy_rows = lax.dynamic_slice_in_dim(vir_energy, aux_index * row_count, row_count, 1)
-    denominator = energy_rows[:, :, None] + vir_energy[:, None, :] - occ_sum[:, None, None]
-    updated = (
-        amplitudes.astype(jnp.float32) - (cycle_term + k_term.astype(jnp.float32)) / denominator
-    )
+    updated = prior - cycle_term * inverse
     return updated.astype(jnp.bfloat16)
 
 

time: 245 us -> 236 us (0.963)
  blocking collectives: 0 us -> 137 us
  waiting for transfers between devices: 149 us -> 30.4 us
  starting transfers between devices: 24.9 us -> 0.1 us
  matrix products: 47.9 us -> 41.9 us
  other arithmetic: 0.58 us -> 6 us
    all_to_all x0 -> x2, blocking collectives: none -> 137 us  [the longest x1 74.3 us: local(): incoming = lax.all_to_all(outgoing, 'pair', 0, 0, tiled=True)]
    all_to_all x2 -> x0, waiting for transfers between devices: 110 us -> none  [the longest x1 59.4 us: local(): incoming = lax.all_to_all(outgoing, 'pair', 0, 0, tiled=True)]
    all_to_all x2 -> x0, starting transfers between devices: 24.8 us -> none  [the longest x1 15 us: local(): incoming = lax.all_to_all(outgoing, 'pair', 0, 0, tiled=True)]
    all_gather x1, waiting for transfers between devices: 38.4 us -> 29.7 us  [local(): lax.all_gather(factors[0], ('pair', 'aux'), axis=0, tiled=True)]
    dot_general x1, matrix products: 15.8 us -> 8.64 us  [local(): jnp.einsum('pca,pba->pcb', own_cycle, margin, preferred_element_type=jnp....]
    div x0 -> x1, other arithmetic: none -> 4.68 us  [local(): inverse = 1.0 / denominator]
    dot_general x1 -> x0, local copies, waits for them, and re-layouts: 2.67 us -> none  [local(): jnp.einsum('jp,pcb->jcb', owner_pick, rotated, preferred_element_type=jnp...]
  transfers between devices with their start and end apart: 4 -> 2, of which waited for: 4 -> 1; matrix products, arithmetic and copies ran while one was open for 11% -> 14% of each run, Pallas kernels for 0% -> 0%
where the time goes in v3:
time: 236 us
  blocking collectives  137 us (58%)
  matrix products  41.9 us (18%)
  waiting for transfers between devices  30.4 us (13%)
  between operations  13.5 us (6%)
  local copies, waits for them, and re-layouts  7.58 us (3%)
  other arithmetic  6 us (3%)
    all_to_all x1, blocking collectives, local(): incoming = lax.all_to_all(outgoing, 'pair', 0, 0, tiled=True)  74.3 us
    all_to_all x1, blocking collectives, local(): returned = lax.all_to_all(slot_back, 'pair', 0, 0, tiled=True)  62.3 us
    all_gather x1, waiting for transfers between devices, local(): lax.all_gather(factors[0], ('pair', 'aux'), axis=0, tiled=True)  29.7 us
    dot_general x1, matrix products, local(): jnp.einsum('pac,pab->pcb', margin, halfway, preferred_element_type=jnp.fl...  14.8 us
    dot_general x1, matrix products, local(): jnp.dot(dressed, own_factors, preferred_element_type=jnp.float32)  11 us
    dot_general x1, matrix products, local(): jnp.einsum('pca,pba->pcb', own_cycle, margin, preferred_element_type=jnp....  8.64 us
  transfers between devices with their start and end apart: 2, of which 1 were waited for; matrix products, arithmetic and copies ran while one was open for 14% of the time, Pallas kernels for 0%

profile of v3, /device:TPU:32, one launch (start us, length us, event | category | flops | bytes accessed | tf_op | source)
XLA Modules:
  0.0 236.1 jit_solution(10337765376204548716)
XLA Ops:
  6.5 0.0 copy-start
  6.5 0.0 all-gather.3.cloned.1.call-start
  6.5 0.7 all-gather.3.cloned.1.call-update
  7.3 0.1 collective-permute-start
  7.4 0.7 fusion.46
  8.0 1.6 gather_fusion
  9.6 1.2 dynamic_slice.15
  10.9 1.1 constant_dynamic-slice_fusion
  11.9 0.7 broadcast_add_fusion
  12.6 0.0 copy-done
  12.6 3.9 %convolution_convert_fusion = bf16[128,128,128]{2,0,1:T(8,128)(2,1)} fusion(bf16[8,128,128]{2,1,0:T(8,128)(2,1)S(1)} %copy-done, s32[128]{0:T(128)} %param.11), kind=kOutput, calls=%fused_computation.19 | convolution fusion | flops 35652608 | bytes 4456960 | tf_op jit(solution)/shard_map/po,oab->pab/dot_general | solution.py:32
  16.5 4.7 %subtract_divide_fusion = (f32[128,64,128]{2,1,0:T(8,128)}, f32[128,64,128]{2,1,0:T(8,128)}) fusion(f32[128]{0:T(128)S(1)} %broadcast_add_fusion, f32[128,128]{1,0:T(8,128)S(1)} %copy-done.5, f32[128,64]{1,0:T(8,128)S(1)} %constant_dynamic-slice_fusion, bf16[128,64,128]{2,1,0:T(8,128)(2,1)S(1)} %copy-done.3, bf16[128,64,128]{2,1,0:T(8,128)(2,1)S(1)} %copy-done.4), kind=kLoop, calls=%fused_computation.11 | loop fusion | flops 7340032 | bytes 12681728 | tf_op jit(solution)/shard_map/div | solution.py:52
  21.2 0.0 collective-permute-done
  21.2 14.8 %fusion.6 = bf16[128,128,128]{2,1,0:T(8,128)(2,1)} fusion(bf16[128,128,128]{2,0,1:T(8,128)(2,1)} %convolution_convert_fusion, bf16[128,64,128]{2,1,0:T(8,128)(2,1)} %collective-permute-done, bf16[128,64,128]{2,1,0:T(8,128)(2,1)} %param.8, pred[]{:T(512)S(6)} %eq.38), kind=kOutput, calls=%fused_computation.12 | convolution fusion | flops 1094713344 | bytes 12582913 | tf_op jit(solution)/shard_map/pac,pab->pcb/dot_general | solution.py:38
  36.0 1.8 dynamic-slice_convert_fusion
  37.8 1.8 fusion.22
  39.6 1.4 copy.26
  41.0 74.3 %all_to_all.10 = bf16[128,64,128]{2,1,0:T(8,128)(2,1)S(1)} all-to-all(bf16[128,64,128]{2,1,0:T(8,128)(2,1)S(1)} %copy.26), channel_id=1, replica_groups=mesh['pair'=128,'aux'=2] {'pair'}, dimensions={0} | all-to-all | bytes 4194304 | tf_op jit(solution)/shard_map/all_to_all | solution.py:55
  115.3 29.7 %all-gather.3.cloned.1.call-done = bf16[1,65536,128]{2,1,0:T(8,128)(2,1)} async-done(((bf16[1,256,128]{2,1,0:T(8,128)(2,1)}), bf16[1,65536,128]{2,1,0:T(8,128)(2,1)}) %all-gather.3.cloned.1.call-update) | async-done | bytes 16777232 | tf_op jit(solution)/shard_map/all_gather | solution.py:20
  145.0 11.0 %fusion.33 = bf16[64,128]{1,0:T(8,128)(2,1)S(1)} fusion(bf16[128,64,128]{2,1,0:T(8,128)(2,1)S(1)} %all_to_all.10, bf16[128,512,128]{2,1,0:T(8,128)(2,1)} %bitcast.24, s32[]{:T(128)S(6)} %select_n.24), kind=kOutput, calls=%fused_computation.30 | convolution fusion | flops 1082179584 | bytes 19021828 | tf_op jit(solution)/shard_map/dot_general | solution.py:59
  156.0 0.5 broadcast_in_dim.2
  156.6 62.3 %all_to_all.11 = bf16[128,64,128]{2,1,0:T(8,128)(2,1)S(1)} all-to-all(bf16[128,64,128]{2,1,0:T(8,128)(2,1)S(1)} %broadcast_in_dim.2), channel_id=1, replica_groups=mesh['pair'=128,'aux'=2] {'pair'}, dimensions={0} | all-to-all | bytes 4194304 | tf_op jit(solution)/shard_map/all_to_all | solution.py:62
  218.9 1.7 fusion.25
  220.6 8.6 %subtract_convert_fusion = bf16[128,64,128]{2,1,0:T(8,128)(2,1)} fusion(f32[128,64,128]{2,1,0:T(8,128)} %get-tuple-element.8, f32[128,64,128]{2,1,0:T(8,128)S(1)} %copy-done.2, bf16[128,128,128]{2,0,1:T(8,128)(2,1)S(1)} %copy-done.1, bf16[128,64,128]{2,0,1:T(8,128)(2,1)S(1)} %fusion.25), kind=kOutput, calls=%fused_computation.9 | convolution fusion | flops 271581184 | bytes 16777216 | tf_op jit(solution)/shard_map/pca,pba->pcb/dot_general | solution.py:66
  (13 shorter events, 0.0 us)
Async XLA Ops:
  6.5 6.1 %copy-start = (bf16[8,128,128]{2,1,0:T(8,128)(2,1)S(1)}, bf16[8,128,128]{2,1,0:T(8,128)(2,1)}, u32[]{:S(2)}) copy-start(bf16[8,128,128]{2,1,0:T(8,128)(2,1)} %param.10) | copy-start | bytes 786436
  6.5 10.0 %copy-start.5 = (f32[128,128]{1,0:T(8,128)S(1)}, f32[128,128]{1,0:T(8,128)}, u32[]{:S(2)}) copy-start(f32[128,128]{1,0:T(8,128)} %param.13) | copy-start | bytes 196612
  6.5 10.0 %copy-start.3 = (bf16[128,64,128]{2,1,0:T(8,128)(2,1)S(1)}, bf16[128,64,128]{2,1,0:T(8,128)(2,1)}, u32[]{:S(2)}) copy-start(bf16[128,64,128]{2,1,0:T(8,128)(2,1)} %param.9) | copy-start | bytes 6291460
  6.5 138.5 %all-gather.3.cloned.1.call-start = ((), (), s32[]{:S(2)}) async-start(), calls=%async_computation.2 | async-start | bytes 16842752 | tf_op jit(solution)/shard_map/all_gather | solution.py:20
  7.3 14.0 %collective-permute-start = (bf16[128,64,128]{2,1,0:T(8,128)(2,1)}, bf16[128,64,128]{2,1,0:T(8,128)(2,1)}, u32[]{:S(2)}, u32[]{:S(2)}) collective-permute-start(bf16[128,64,128]{2,1,0:T(8,128)(2,1)} %param.8), channel_id=1, source_target_pairs={{0,1},{1,0},{2,3},{3,2},{4,5},{5,4},{6,7},{7,6},{8,9},{9,8},{10,11... | collective-permute-start | bytes 6291464 | tf_op jit(solution)/shard_map/ppermute | solution.py:23
  10.9 5.7 %copy-start.4 = (bf16[128,64,128]{2,1,0:T(8,128)(2,1)S(1)}, bf16[128,64,128]{2,1,0:T(8,128)(2,1)}, u32[]{:S(2)}) copy-start(bf16[128,64,128]{2,1,0:T(8,128)(2,1)} %param.8) | copy-start | bytes 6291460
  36.0 1.8 copy-start.6
  156.6 64.1 %copy-start.1 = (bf16[128,128,128]{2,0,1:T(8,128)(2,1)S(1)}, bf16[128,128,128]{2,0,1:T(8,128)(2,1)}, u32[]{:S(2)}) copy-start(bf16[128,128,128]{2,0,1:T(8,128)(2,1)} %convolution_convert_fusion) | copy-start | bytes 12582916
  156.6 64.1 %copy-start.2 = (f32[128,64,128]{2,1,0:T(8,128)S(1)}, f32[128,64,128]{2,1,0:T(8,128)}, u32[]{:S(2)}) copy-start(f32[128,64,128]{2,1,0:T(8,128)} %get-tuple-element.10) | copy-start | bytes 12582916
Sparse Core Ops, SparseCore 0:
  11.0 133.9 all-gather.2

commit v4 on v3

--- a/solution.py
+++ b/solution.py
@@ -2,6 +2,20 @@
 import jax.numpy as jnp
 from jax import lax
 from jax.sharding import PartitionSpec as P
+
+
+RING_ORDER = ((8, 4), (4, 1), (4, 32))
+
+
+def ring_gather(block, size, stride, total):
+    pieces = [block]
+    for shift in range(1, size):
+        perm = []
+        for device in range(total):
+            coord = (device // stride) % size
+            perm.append((device, device + ((coord + shift) % size - coord) * stride))
+        pieces.append(lax.ppermute(block, "pair", perm))
+    return jnp.stack(pieces)
 
 
 def local(
@@ -58,10 +72,21 @@
     ).astype(jnp.bfloat16)
     local_cycle = jnp.dot(dressed, own_factors, preferred_element_type=jnp.float32)
     cycle_vals = (cycle_scale * local_cycle).astype(jnp.bfloat16)
-    slot_back = jnp.broadcast_to(cycle_vals[None], (axis_pairs, row_count, vir_width))
-    returned = lax.all_to_all(slot_back, "pair", 0, 0, tiled=True)
+    returned = cycle_vals
+    ring_offset = jnp.zeros_like(pair_dest)
+    ring_scale = 1
+    for size, stride in RING_ORDER:
+        returned = ring_gather(returned, size, stride, axis_pairs)
+        own_coord = (own_index // stride) % size
+        dest_coord = (pair_dest // stride) % size
+        ring_offset = ring_offset + ((own_coord - dest_coord) % size) * ring_scale
+        ring_scale = ring_scale * size
+    returned = returned.reshape(axis_pairs, row_count, vir_width)
+    offset_pick = (
+        jnp.arange(axis_pairs, dtype=jnp.int32)[:, None] == ring_offset[None, :]
+    ).astype(jnp.bfloat16)
     own_cycle = jnp.einsum(
-        "jp,jca->pca", owner_pick, returned, preferred_element_type=jnp.float32
+        "jp,jca->pca", offset_pick, returned, preferred_element_type=jnp.float32
     ).astype(jnp.bfloat16)
     cycle_term = jnp.einsum("pca,pba->pcb", own_cycle, margin, preferred_element_type=jnp.float32)
     updated = prior - cycle_term * inverse

time: 236 us -> 225 us (0.953)
  blocking collectives: 137 us -> 74.3 us
  starting transfers between devices: 0.1 us -> 24.7 us
  waiting for transfers between devices: 30.4 us -> 53.7 us
    all_to_all x1 -> x0, blocking collectives: 62.3 us -> none  [local(): returned = lax.all_to_all(slot_back, 'pair', 0, 0, tiled=True)]
    ppermute x0 -> x13, starting transfers between devices: none -> 24.6 us  [ring_gather(): pieces.append(lax.ppermute(block, 'pair', perm))]
    ppermute x0 -> x13, waiting for transfers between devices: none -> 24.3 us  [ring_gather(): pieces.append(lax.ppermute(block, 'pair', perm))]
  transfers between devices with their start and end apart: 2 -> 15, of which waited for: 1 -> 9; matrix products, arithmetic and copies ran while one was open for 14% -> 15% of each run, Pallas kernels for 0% -> 0%
where the time goes in v4:
time: 225 us; the launch traced here: 223 us
  blocking collectives  74.3 us (33%)
  waiting for transfers between devices  53.7 us (24%)
  matrix products  42 us (19%)
  starting transfers between devices  24.7 us (11%)
  between operations  13.5 us (6%)
  local copies, waits for them, and re-layouts  8.56 us (4%)
  other arithmetic  6.47 us (3%)
    all_to_all x1, blocking collectives, local(): incoming = lax.all_to_all(outgoing, 'pair', 0, 0, tiled=True)  74.3 us
    all_gather x1, waiting for transfers between devices, local(): lax.all_gather(factors[0], ('pair', 'aux'), axis=0, tiled=True)  28.7 us
    ppermute x13, starting transfers between devices, ring_gather(): pieces.append(lax.ppermute(block, 'pair', perm))  24.6 us
    ppermute x13, waiting for transfers between devices, ring_gather(): pieces.append(lax.ppermute(block, 'pair', perm))  24.3 us
    dot_general x1, matrix products, local(): jnp.einsum('pac,pab->pcb', margin, halfway, preferred_element_type=jnp.fl...  14.9 us
    dot_general x1, matrix products, local(): jnp.dot(dressed, own_factors, preferred_element_type=jnp.float32)  11 us
    dot_general x1, matrix products, local(): jnp.einsum('pca,pba->pcb', own_cycle, margin, preferred_element_type=jnp....  8.63 us
    div x1, other arithmetic, local(): inverse = 1.0 / denominator  4.77 us
  transfers between devices with their start and end apart: 15, of which 9 were waited for; matrix products, arithmetic and copies ran while one was open for 15% of the time, Pallas kernels for 0%

profile of v4, /device:TPU:32, one launch (start us, length us, event | category | flops | bytes accessed | tf_op | source)
XLA Modules:
  0.0 223.2 jit_solution(11171059530084323425)
XLA Ops:
  9.3 1.6 gather_fusion
  12.6 3.9 %convolution_convert_fusion = bf16[128,128,128]{2,0,1:T(8,128)(2,1)} fusion(bf16[8,128,128]{2,1,0:T(8,128)(2,1)S(1)} %copy-done, s32[128]{0:T(128)} %param.11), kind=kOutput, calls=%fused_computation.19 | convolution fusion | flops 35652608 | bytes 4456960 | tf_op jit(solution)/shard_map/po,oab->pab/dot_general | solution.py:46
  16.6 4.8 %subtract_divide_fusion = (f32[128,64,128]{2,1,0:T(8,128)}, f32[128,64,128]{2,1,0:T(8,128)}) fusion(f32[128]{0:T(128)S(1)} %broadcast_add_fusion, f32[128,128]{1,0:T(8,128)S(1)} %copy-done.5, f32[128,64]{1,0:T(8,128)S(1)} %constant_dynamic-slice_fusion, bf16[128,64,128]{2,1,0:T(8,128)(2,1)S(1)} %copy-done.3, bf16[128,64,128]{2,1,0:T(8,128)(2,1)S(1)} %copy-done.4), kind=kLoop, calls=%fused_computation.11 | loop fusion | flops 7340032 | bytes 12681728 | tf_op jit(solution)/shard_map/div | solution.py:66
  21.3 14.9 %fusion.6 = bf16[128,128,128]{2,1,0:T(8,128)(2,1)} fusion(bf16[128,128,128]{2,0,1:T(8,128)(2,1)} %convolution_convert_fusion, bf16[128,64,128]{2,1,0:T(8,128)(2,1)} %collective-permute-done, bf16[128,64,128]{2,1,0:T(8,128)(2,1)} %param.8, pred[]{:T(512)S(6)} %eq.62), kind=kOutput, calls=%fused_computation.12 | convolution fusion | flops 1094713344 | bytes 12582913 | tf_op jit(solution)/shard_map/pac,pab->pcb/dot_general | solution.py:52
  36.2 1.8 dynamic-slice_convert_fusion
  38.0 1.8 fusion.22
  41.1 74.3 %all_to_all.5 = bf16[128,64,128]{2,1,0:T(8,128)(2,1)S(1)} all-to-all(bf16[128,64,128]{2,1,0:T(8,128)(2,1)S(1)} %copy.17), channel_id=1, replica_groups=mesh['pair'=128,'aux'=2] {'pair'}, dimensions={0} | all-to-all | bytes 4194304 | tf_op jit(solution)/shard_map/all_to_all | solution.py:69
  115.5 28.7 %all-gather.3.cloned.1.call-done = bf16[1,65536,128]{2,1,0:T(8,128)(2,1)} async-done(((bf16[1,256,128]{2,1,0:T(8,128)(2,1)}), bf16[1,65536,128]{2,1,0:T(8,128)(2,1)}) %all-gather.3.cloned.1.call-update) | async-done | bytes 16777232 | tf_op jit(solution)/shard_map/all_gather | solution.py:34
  144.2 11.0 %constant_dynamic-update-slice_fusion.7 = (bf16[8,64,128]{2,1,0:T(8,128)(2,1)S(1)}, bf16[64,128]{1,0:T(8,128)(2,1)S(1)}) fusion(bf16[128,512,128]{2,1,0:T(8,128)(2,1)} %bitcast.56, s32[]{:T(128)S(6)} %select_n.115, bf16[128,64,128]{2,1,0:T(8,128)(2,1)S(1)} %all_to_all.5), kind=kOutput, calls=%fused_computation.49 | convolution fusion | flops 1082179584 | bytes 19038212 | tf_op jit(solution)/shard_map/dot_general | solution.py:73
  155.2 1.7 collective-permute-start.1
  157.0 2.0 collective-permute-start.2
  159.0 1.6 collective-permute-start.3
  160.6 3.4 %collective-permute-start.4 = (bf16[64,128]{1,0:T(8,128)(2,1)S(1)}, bf16[64,128]{1,0:T(8,128)(2,1)S(1)}, u32[]{:S(2)}, u32[]{:S(2)}) collective-permute-start(bf16[64,128]{1,0:T(8,128)(2,1)S(1)} %get-tuple-element.16), channel_id=1, source_target_pairs={{0,32},{2,34},{4,36},{6,38},{8,40},{10,42},{12,44},{14,46},{16,48}... | collective-permute-start | bytes 49160 | tf_op jit(solution)/shard_map/ppermute | solution.py:17
  164.0 2.7 %collective-permute-start.5 = (bf16[64,128]{1,0:T(8,128)(2,1)S(1)}, bf16[64,128]{1,0:T(8,128)(2,1)S(1)}, u32[]{:S(2)}, u32[]{:S(2)}) collective-permute-start(bf16[64,128]{1,0:T(8,128)(2,1)S(1)} %get-tuple-element.16), channel_id=1, source_target_pairs={{0,40},{2,42},{4,44},{6,46},{8,48},{10,50},{12,52},{14,54},{16,56}... | collective-permute-start | bytes 49160 | tf_op jit(solution)/shard_map/ppermute | solution.py:17
  167.6 2.1 collective-permute-start.7
  172.8 2.9 %collective-permute-start.9 = (bf16[8,64,128]{2,1,0:T(8,128)(2,1)S(1)}, bf16[8,64,128]{2,1,0:T(8,128)(2,1)S(1)}, u32[]{:S(2)}, u32[]{:S(2)}) collective-permute-start(bf16[8,64,128]{2,1,0:T(8,128)(2,1)S(1)} %constant_dynamic-update-slice_fusion), channel_id=1, source_target_pairs={{0,4},{2,6},{4,0},{6,2},{8,12},{10,14},{12,8},{14,10},{16,20},{18,... | collective-permute-start | bytes 393224 | tf_op jit(solution)/shard_map/ppermute | solution.py:17
  176.8 1.6 collective-permute-done.8
  178.5 1.6 collective-permute-done.9
  181.4 2.8 %collective-permute-start.12 = (bf16[4,8,64,128]{3,2,1,0:T(8,128)(2,1)S(1)}, bf16[4,8,64,128]{3,2,1,0:T(8,128)(2,1)S(1)}, u32[]{:S(2)}, u32[]{:S(2)}) collective-permute-start(bf16[4,8,64,128]{3,2,1,0:T(8,128)(2,1)S(1)} %get-tuple-element.12), channel_id=1, source_target_pairs={{0,128},{2,130},{4,132},{6,134},{8,136},{10,138},{12,140},{14,142}... | collective-permute-start | bytes 1572872 | tf_op jit(solution)/shard_map/ppermute | solution.py:17
  184.2 1.4 collective-permute-start.13
  185.6 10.6 %collective-permute-done.11 = bf16[4,8,64,128]{3,2,1,0:T(8,128)(2,1)S(1)} collective-permute-done((bf16[4,8,64,128]{3,2,1,0:T(8,128)(2,1)S(1)}, bf16[4,8,64,128]{3,2,1,0:T(8,128)(2,1)S(1)}, u32[]{:S(2)}, u32[]{:S(2)}) %collective-permute-start.11) | collective-permute-done | bytes 524320 | tf_op jit(solution)/shard_map/ppermute | solution.py:17
  196.3 7.8 %collective-permute-done.12 = bf16[4,8,64,128]{3,2,1,0:T(8,128)(2,1)S(1)} collective-permute-done((bf16[4,8,64,128]{3,2,1,0:T(8,128)(2,1)S(1)}, bf16[4,8,64,128]{3,2,1,0:T(8,128)(2,1)S(1)}, u32[]{:S(2)}, u32[]{:S(2)}) %collective-permute-start.12) | collective-permute-done | bytes 524320 | tf_op jit(solution)/shard_map/ppermute | solution.py:17
  204.6 1.7 fusion.25
  207.8 8.6 %subtract_convert_fusion = bf16[128,64,128]{2,1,0:T(8,128)(2,1)} fusion(f32[128,64,128]{2,1,0:T(8,128)} %get-tuple-element.8, f32[128,64,128]{2,1,0:T(8,128)S(1)} %copy-done.2, bf16[128,128,128]{2,0,1:T(8,128)(2,1)S(1)} %copy-done.1, bf16[128,64,128]{2,0,1:T(8,128)(2,1)S(1)} %fusion.25), kind=kOutput, calls=%fused_computation.9 | convolution fusion | flops 271581184 | bytes 16777216 | tf_op jit(solution)/shard_map/pca,pba->pcb/dot_general | solution.py:91
  (47 shorter events, 14.3 us)
Async XLA Ops:
  6.5 6.1 %copy-start = (bf16[8,128,128]{2,1,0:T(8,128)(2,1)S(1)}, bf16[8,128,128]{2,1,0:T(8,128)(2,1)}, u32[]{:S(2)}) copy-start(bf16[8,128,128]{2,1,0:T(8,128)(2,1)} %param.10) | copy-start | bytes 786436
  6.5 10.0 %copy-start.5 = (f32[128,128]{1,0:T(8,128)S(1)}, f32[128,128]{1,0:T(8,128)}, u32[]{:S(2)}) copy-start(f32[128,128]{1,0:T(8,128)} %param.13) | copy-start | bytes 196612
  6.5 10.0 %copy-start.3 = (bf16[128,64,128]{2,1,0:T(8,128)(2,1)S(1)}, bf16[128,64,128]{2,1,0:T(8,128)(2,1)}, u32[]{:S(2)}) copy-start(bf16[128,64,128]{2,1,0:T(8,128)(2,1)} %param.9) | copy-start | bytes 6291460
  6.5 137.7 %all-gather.3.cloned.1.call-start = ((), (), s32[]{:S(2)}) async-start(), calls=%async_computation.1 | async-start | bytes 16842752 | tf_op jit(solution)/shard_map/all_gather | solution.py:34
  7.3 14.1 %collective-permute-start = (bf16[128,64,128]{2,1,0:T(8,128)(2,1)}, bf16[128,64,128]{2,1,0:T(8,128)(2,1)}, u32[]{:S(2)}, u32[]{:S(2)}) collective-permute-start(bf16[128,64,128]{2,1,0:T(8,128)(2,1)} %param.8), channel_id=1, source_target_pairs={{0,1},{1,0},{2,3},{3,2},{4,5},{5,4},{6,7},{7,6},{8,9},{9,8},{10,11... | collective-permute-start | bytes 6291464 | tf_op jit(solution)/shard_map/ppermute | solution.py:37
  10.9 5.7 %copy-start.4 = (bf16[128,64,128]{2,1,0:T(8,128)(2,1)S(1)}, bf16[128,64,128]{2,1,0:T(8,128)(2,1)}, u32[]{:S(2)}) copy-start(bf16[128,64,128]{2,1,0:T(8,128)(2,1)} %param.8) | copy-start | bytes 6291460
  36.2 1.8 copy-start.6
  155.2 11.5 %collective-permute-start.1 = (bf16[64,128]{1,0:T(8,128)(2,1)S(1)}, bf16[64,128]{1,0:T(8,128)(2,1)S(1)}, u32[]{:S(2)}, u32[]{:S(2)}) collective-permute-start(bf16[64,128]{1,0:T(8,128)(2,1)S(1)} %get-tuple-element.16), channel_id=1, source_target_pairs={{0,8},{2,10},{4,12},{6,14},{8,16},{10,18},{12,20},{14,22},{16,24},... | collective-permute-start | bytes 49160 | tf_op jit(solution)/shard_map/ppermute | solution.py:17
  157.0 10.6 %collective-permute-start.2 = (bf16[64,128]{1,0:T(8,128)(2,1)S(1)}, bf16[64,128]{1,0:T(8,128)(2,1)S(1)}, u32[]{:S(2)}, u32[]{:S(2)}) collective-permute-start(bf16[64,128]{1,0:T(8,128)(2,1)S(1)} %get-tuple-element.16), channel_id=1, source_target_pairs={{0,16},{2,18},{4,20},{6,22},{8,24},{10,26},{12,28},{14,30},{16,32}... | collective-permute-start | bytes 49160 | tf_op jit(solution)/shard_map/ppermute | solution.py:17
  159.0 10.7 %collective-permute-start.3 = (bf16[64,128]{1,0:T(8,128)(2,1)S(1)}, bf16[64,128]{1,0:T(8,128)(2,1)S(1)}, u32[]{:S(2)}, u32[]{:S(2)}) collective-permute-start(bf16[64,128]{1,0:T(8,128)(2,1)S(1)} %get-tuple-element.16), channel_id=1, source_target_pairs={{0,24},{2,26},{4,28},{6,30},{8,32},{10,34},{12,36},{14,38},{16,40}... | collective-permute-start | bytes 49160 | tf_op jit(solution)/shard_map/ppermute | solution.py:17
  160.6 9.0 %collective-permute-start.4 = (bf16[64,128]{1,0:T(8,128)(2,1)S(1)}, bf16[64,128]{1,0:T(8,128)(2,1)S(1)}, u32[]{:S(2)}, u32[]{:S(2)}) collective-permute-start(bf16[64,128]{1,0:T(8,128)(2,1)S(1)} %get-tuple-element.16), channel_id=1, source_target_pairs={{0,32},{2,34},{4,36},{6,38},{8,40},{10,42},{12,44},{14,46},{16,48}... | collective-permute-start | bytes 49160 | tf_op jit(solution)/shard_map/ppermute | solution.py:17
  164.0 6.8 %collective-permute-start.5 = (bf16[64,128]{1,0:T(8,128)(2,1)S(1)}, bf16[64,128]{1,0:T(8,128)(2,1)S(1)}, u32[]{:S(2)}, u32[]{:S(2)}) collective-permute-start(bf16[64,128]{1,0:T(8,128)(2,1)S(1)} %get-tuple-element.16), channel_id=1, source_target_pairs={{0,40},{2,42},{4,44},{6,46},{8,48},{10,50},{12,52},{14,54},{16,56}... | collective-permute-start | bytes 49160 | tf_op jit(solution)/shard_map/ppermute | solution.py:17
  166.7 4.7 %collective-permute-start.6 = (bf16[64,128]{1,0:T(8,128)(2,1)S(1)}, bf16[64,128]{1,0:T(8,128)(2,1)S(1)}, u32[]{:S(2)}, u32[]{:S(2)}) collective-permute-start(bf16[64,128]{1,0:T(8,128)(2,1)S(1)} %get-tuple-element.16), channel_id=1, source_target_pairs={{0,48},{2,50},{4,52},{6,54},{8,56},{10,58},{12,60},{14,62},{16,0},... | collective-permute-start | bytes 49160 | tf_op jit(solution)/shard_map/ppermute | solution.py:17
  167.6 3.9 %collective-permute-start.7 = (bf16[64,128]{1,0:T(8,128)(2,1)S(1)}, bf16[64,128]{1,0:T(8,128)(2,1)S(1)}, u32[]{:S(2)}, u32[]{:S(2)}) collective-permute-start(bf16[64,128]{1,0:T(8,128)(2,1)S(1)} %get-tuple-element.16), channel_id=1, source_target_pairs={{0,56},{2,58},{4,60},{6,62},{8,0},{10,2},{12,4},{14,6},{16,8},{18,... | collective-permute-start | bytes 49160 | tf_op jit(solution)/shard_map/ppermute | solution.py:17
  171.5 7.0 %collective-permute-start.8 = (bf16[8,64,128]{2,1,0:T(8,128)(2,1)S(1)}, bf16[8,64,128]{2,1,0:T(8,128)(2,1)S(1)}, u32[]{:S(2)}, u32[]{:S(2)}) collective-permute-start(bf16[8,64,128]{2,1,0:T(8,128)(2,1)S(1)} %constant_dynamic-update-slice_fusion), channel_id=1, source_target_pairs={{0,2},{2,4},{4,6},{6,0},{8,10},{10,12},{12,14},{14,8},{16,18},{18,... | collective-permute-start | bytes 393224 | tf_op jit(solution)/shard_map/ppermute | solution.py:17
  172.8 7.2 %collective-permute-start.9 = (bf16[8,64,128]{2,1,0:T(8,128)(2,1)S(1)}, bf16[8,64,128]{2,1,0:T(8,128)(2,1)S(1)}, u32[]{:S(2)}, u32[]{:S(2)}) collective-permute-start(bf16[8,64,128]{2,1,0:T(8,128)(2,1)S(1)} %constant_dynamic-update-slice_fusion), channel_id=1, source_target_pairs={{0,4},{2,6},{4,0},{6,2},{8,12},{10,14},{12,8},{14,10},{16,20},{18,... | collective-permute-start | bytes 393224 | tf_op jit(solution)/shard_map/ppermute | solution.py:17
  175.7 5.0 %collective-permute-start.10 = (bf16[8,64,128]{2,1,0:T(8,128)(2,1)S(1)}, bf16[8,64,128]{2,1,0:T(8,128)(2,1)S(1)}, u32[]{:S(2)}, u32[]{:S(2)}) collective-permute-start(bf16[8,64,128]{2,1,0:T(8,128)(2,1)S(1)} %constant_dynamic-update-slice_fusion), channel_id=1, source_target_pairs={{0,6},{2,0},{4,2},{6,4},{8,14},{10,8},{12,10},{14,12},{16,22},{18,... | collective-permute-start | bytes 393224 | tf_op jit(solution)/shard_map/ppermute | solution.py:17
  180.7 15.5 %collective-permute-start.11 = (bf16[4,8,64,128]{3,2,1,0:T(8,128)(2,1)S(1)}, bf16[4,8,64,128]{3,2,1,0:T(8,128)(2,1)S(1)}, u32[]{:S(2)}, u32[]{:S(2)}) collective-permute-start(bf16[4,8,64,128]{3,2,1,0:T(8,128)(2,1)S(1)} %get-tuple-element.12), channel_id=1, source_target_pairs={{0,64},{2,66},{4,68},{6,70},{8,72},{10,74},{12,76},{14,78},{16,80}... | collective-permute-start | bytes 1572872 | tf_op jit(solution)/shard_map/ppermute | solution.py:17
  181.4 22.6 %collective-permute-start.12 = (bf16[4,8,64,128]{3,2,1,0:T(8,128)(2,1)S(1)}, bf16[4,8,64,128]{3,2,1,0:T(8,128)(2,1)S(1)}, u32[]{:S(2)}, u32[]{:S(2)}) collective-permute-start(bf16[4,8,64,128]{3,2,1,0:T(8,128)(2,1)S(1)} %get-tuple-element.12), channel_id=1, source_target_pairs={{0,128},{2,130},{4,132},{6,134},{8,136},{10,138},{12,140},{14,142}... | collective-permute-start | bytes 1572872 | tf_op jit(solution)/shard_map/ppermute | solution.py:17
  184.2 20.1 %collective-permute-start.13 = (bf16[4,8,64,128]{3,2,1,0:T(8,128)(2,1)S(1)}, bf16[4,8,64,128]{3,2,1,0:T(8,128)(2,1)S(1)}, u32[]{:S(2)}, u32[]{:S(2)}) collective-permute-start(bf16[4,8,64,128]{3,2,1,0:T(8,128)(2,1)S(1)} %get-tuple-element.12), channel_id=1, source_target_pairs={{0,192},{2,194},{4,196},{6,198},{8,200},{10,202},{12,204},{14,206}... | collective-permute-start | bytes 1572872 | tf_op jit(solution)/shard_map/ppermute | solution.py:17
  204.3 2.2 copy-start.1
  204.3 3.5 %copy-start.2 = (f32[128,64,128]{2,1,0:T(8,128)S(1)}, f32[128,64,128]{2,1,0:T(8,128)}, u32[]{:S(2)}) copy-start(f32[128,64,128]{2,1,0:T(8,128)} %get-tuple-element.10) | copy-start | bytes 12582916
Sparse Core Ops, SparseCore 0:
  11.0 133.1 all-gather.2

commit v5 on v4

--- a/solution.py
+++ b/solution.py
@@ -31,10 +31,10 @@
     aux_rows = factors.shape[1]
     ovl_count = margin_table.shape[0]
     cycle_scale = float(vir_width * aux_rows * aux_count * pair_count) ** (-0.5)
-    every_factor = lax.all_gather(factors[0], ("pair", "aux"), axis=0, tiled=True)
-    every_factor = every_factor.reshape(axis_pairs, aux_count * aux_rows, vir_width)
-    own_factors = lax.dynamic_index_in_dim(every_factor, own_index, 0, keepdims=False)
-    other_amp = lax.ppermute(amplitudes, "aux", perm=[(0, 1), (1, 0)])
+    every_factor = lax.all_gather(factors[0], "pair", axis=0, tiled=True)
+    every_factor = every_factor.reshape(axis_pairs, aux_rows, vir_width)
+    swap = [(0, 1), (1, 0)]
+    other_amp = lax.ppermute(amplitudes, "aux", perm=swap)
     full_amp = jnp.where(
         aux_index == 0,
         jnp.concatenate([amplitudes, other_amp], axis=1),
@@ -67,10 +67,19 @@
     prior = amplitudes.astype(jnp.float32) - k_term.astype(jnp.float32) * inverse
     outgoing, prior, inverse = lax.optimization_barrier((outgoing, prior, inverse))
     incoming = lax.all_to_all(outgoing, "pair", 0, 0, tiled=True)
+    other_rows = lax.ppermute(incoming, "aux", perm=swap)
+    all_rows = jnp.where(
+        aux_index == 0,
+        jnp.concatenate([incoming, other_rows], axis=1),
+        jnp.concatenate([other_rows, incoming], axis=1),
+    )
     dressed = jnp.einsum(
-        "ica,iqa->cq", incoming, every_factor, preferred_element_type=jnp.float32
+        "ica,iqa->cq", all_rows, every_factor, preferred_element_type=jnp.float32
     ).astype(jnp.bfloat16)
-    local_cycle = jnp.dot(dressed, own_factors, preferred_element_type=jnp.float32)
+    half_cycle = jnp.dot(dressed, factors[0], preferred_element_type=jnp.float32)
+    own_half = lax.dynamic_slice_in_dim(half_cycle, aux_index * row_count, row_count, 0)
+    sent_half = lax.dynamic_slice_in_dim(half_cycle, (1 - aux_index) * row_count, row_count, 0)
+    local_cycle = own_half + lax.ppermute(sent_half, "aux", perm=swap)
     cycle_vals = (cycle_scale * local_cycle).astype(jnp.bfloat16)
     returned = cycle_vals
     ring_offset = jnp.zeros_like(pair_dest)

time: 225 us -> 226 us (level)
  waiting for transfers between devices: 53.7 us -> 61.2 us
  matrix products: 42 us -> 38.7 us
  starting transfers between devices: 24.7 us -> 21.9 us
    ppermute x13, waiting for transfers between devices: 24.3 us -> 31.7 us  [ring_gather(): pieces.append(lax.ppermute(block, 'pair', perm))]
    ppermute x1 -> x3, waiting for transfers between devices: 0.01 us -> 5.49 us  [the longest x1 4.29 us: local(): other_rows = lax.ppermute(incoming, 'aux', perm=swap)]
    all_gather x1, waiting for transfers between devices: 28.7 us -> 23.3 us  [local(): every_factor = lax.all_gather(factors[0], 'pair', axis=0, tiled=True)]
    dot_general x1 -> x2, matrix products: 11 us -> 7.69 us  [the longest x1 7.55 us: local(): jnp.einsum('ica,iqa->cq', all_rows, every_factor, preferred_element_type=...]
    ppermute x13, starting transfers between devices: 24.6 us -> 21.7 us  [ring_gather(): pieces.append(lax.ppermute(block, 'pair', perm))]
  transfers between devices with their start and end apart: 15 -> 17, of which waited for: 9 -> 10; matrix products, arithmetic and copies ran while one was open for 15% -> 15% of each run, Pallas kernels for 0% -> 0%
where the time goes in v5:
time: 226 us; the launch traced here: 225 us
  blocking collectives  74.3 us (33%)
  waiting for transfers between devices  61.2 us (27%)
  matrix products  38.7 us (17%)
  starting transfers between devices  21.9 us (10%)
  between operations  13.6 us (6%)
  local copies, waits for them, and re-layouts  8.58 us (4%)
  other arithmetic  6.4 us (3%)
    all_to_all x1, blocking collectives, local(): incoming = lax.all_to_all(outgoing, 'pair', 0, 0, tiled=True)  74.3 us
    ppermute x13, waiting for transfers between devices, ring_gather(): pieces.append(lax.ppermute(block, 'pair', perm))  31.7 us
    all_gather x1, waiting for transfers between devices, local(): every_factor = lax.all_gather(factors[0], 'pair', axis=0, tiled=True)  23.3 us
    ppermute x13, starting transfers between devices, ring_gather(): pieces.append(lax.ppermute(block, 'pair', perm))  21.7 us
    dot_general x1, matrix products, local(): jnp.einsum('pac,pab->pcb', margin, halfway, preferred_element_type=jnp.fl...  14.9 us
    dot_general x1, matrix products, local(): jnp.einsum('pca,pba->pcb', own_cycle, margin, preferred_element_type=jnp....  8.63 us
    dot_general x1, matrix products, local(): jnp.einsum('ica,iqa->cq', all_rows, every_factor, preferred_element_type=...  7.55 us
    div x1, other arithmetic, local(): inverse = 1.0 / denominator  4.69 us
  transfers between devices with their start and end apart: 17, of which 10 were waited for; matrix products, arithmetic and copies ran while one was open for 15% of the time, Pallas kernels for 0%

profile of v5, /device:TPU:32, one launch (start us, length us, event | category | flops | bytes accessed | tf_op | source)
XLA Modules:
  0.0 224.7 jit_solution(872022748694647981)
XLA Ops:
  9.3 1.6 gather_fusion
  12.6 3.9 %convolution_convert_fusion = bf16[128,128,128]{2,0,1:T(8,128)(2,1)} fusion(bf16[8,128,128]{2,1,0:T(8,128)(2,1)S(1)} %copy-done, s32[128]{0:T(128)} %param.11), kind=kOutput, calls=%fused_computation.27 | convolution fusion | flops 35652608 | bytes 4456960 | tf_op jit(solution)/shard_map/po,oab->pab/dot_general | solution.py:46
  16.5 4.7 %subtract_divide_fusion = (f32[128,64,128]{2,1,0:T(8,128)}, f32[128,64,128]{2,1,0:T(8,128)}) fusion(f32[128]{0:T(128)S(1)} %broadcast_add_fusion, f32[128,128]{1,0:T(8,128)S(1)} %copy-done.5, f32[128,64]{1,0:T(8,128)S(1)} %constant_dynamic-slice_fusion.1, bf16[128,64,128]{2,1,0:T(8,128)(2,1)S(1)} %copy-done.3, bf16[128,64,128]{2,1,0:T(8,128)(2,1)S(1)} %copy-done.4), kind=kLoop, calls=%fused_computation.18 | loop fusion | flops 7340032 | bytes 12681728 | tf_op jit(solution)/shard_map/div | solution.py:66
  21.2 14.9 %fusion.12 = bf16[128,128,128]{2,1,0:T(8,128)(2,1)} fusion(bf16[128,128,128]{2,0,1:T(8,128)(2,1)} %convolution_convert_fusion, bf16[128,64,128]{2,1,0:T(8,128)(2,1)} %collective-permute-done, bf16[128,64,128]{2,1,0:T(8,128)(2,1)} %param.8, pred[]{:T(512)S(6)} %eq.63), kind=kOutput, calls=%fused_computation.19 | convolution fusion | flops 1094713344 | bytes 12582913 | tf_op jit(solution)/shard_map/pac,pab->pcb/dot_general | solution.py:52
  36.2 1.8 dynamic-slice_convert_fusion
  38.0 1.8 fusion.29
  39.7 1.4 copy.23
  41.1 74.3 %all_to_all.5 = bf16[128,64,128]{2,1,0:T(8,128)(2,1)S(1)} all-to-all(bf16[128,64,128]{2,1,0:T(8,128)(2,1)S(1)} %copy.23), channel_id=1, replica_groups=mesh['pair'=128,'aux'=2] {'pair'}, dimensions={0} | all-to-all | bytes 4194304 | tf_op jit(solution)/shard_map/all_to_all | solution.py:69
  115.4 4.3 %collective-permute-done.1 = bf16[128,64,128]{2,1,0:T(8,128)(2,1)} collective-permute-done((bf16[128,64,128]{2,1,0:T(8,128)(2,1)S(1)}, bf16[128,64,128]{2,1,0:T(8,128)(2,1)}, u32[]{:S(2)}, u32[]{:S(2)}) %collective-permute-start.1) | collective-permute-done | bytes 2097184 | tf_op jit(solution)/shard_map/ppermute | solution.py:70
  119.7 23.3 %all-gather.3.cloned.1.call-done = bf16[1,32768,128]{2,1,0:T(8,128)(2,1)} async-done(((bf16[1,256,128]{2,1,0:T(8,128)(2,1)}), bf16[1,32768,128]{2,1,0:T(8,128)(2,1)}) %all-gather.3.cloned.1.call-update) | async-done | bytes 8388624 | tf_op jit(solution)/shard_map/all_gather | solution.py:34
  143.0 7.6 %fusion.40 = bf16[128,256]{1,0:T(8,128)(2,1)S(1)} fusion(bf16[128,256,128]{2,1,0:T(8,128)(2,1)} %bitcast.59, bf16[128,64,128]{2,1,0:T(8,128)(2,1)} %collective-permute-done.1, bf16[128,64,128]{2,1,0:T(8,128)(2,1)S(1)} %all_to_all.5, pred[]{:T(512)S(6)} %eq.63), kind=kOutput, calls=%fused_computation.37 | convolution fusion | flops 1092648960 | bytes 12648449 | tf_op jit(solution)/shard_map/ica,iqa->cq/dot_general | solution.py:76
  152.1 1.4 collective-permute-start.3
  153.4 3.0 %collective-permute-start.8 = (bf16[64,128]{1,0:T(8,128)(2,1)S(1)}, bf16[64,128]{1,0:T(8,128)(2,1)S(1)}, u32[]{:S(2)}, u32[]{:S(2)}) collective-permute-start(bf16[64,128]{1,0:T(8,128)(2,1)S(1)} %get-tuple-element.12), channel_id=1, source_target_pairs={{0,48},{2,50},{4,52},{6,54},{8,56},{10,58},{12,60},{14,62},{16,0},... | collective-permute-start | bytes 49160 | tf_op jit(solution)/shard_map/ppermute | solution.py:17
  157.0 3.2 %collective-permute-start.6 = (bf16[64,128]{1,0:T(8,128)(2,1)S(1)}, bf16[64,128]{1,0:T(8,128)(2,1)S(1)}, u32[]{:S(2)}, u32[]{:S(2)}) collective-permute-start(bf16[64,128]{1,0:T(8,128)(2,1)S(1)} %get-tuple-element.12), channel_id=1, source_target_pairs={{0,32},{2,34},{4,36},{6,38},{8,40},{10,42},{12,44},{14,46},{16,48}... | collective-permute-start | bytes 49160 | tf_op jit(solution)/shard_map/ppermute | solution.py:17
  160.1 3.8 %collective-permute-start.5 = (bf16[64,128]{1,0:T(8,128)(2,1)S(1)}, bf16[64,128]{1,0:T(8,128)(2,1)S(1)}, u32[]{:S(2)}, u32[]{:S(2)}) collective-permute-start(bf16[64,128]{1,0:T(8,128)(2,1)S(1)} %get-tuple-element.12), channel_id=1, source_target_pairs={{0,24},{2,26},{4,28},{6,30},{8,32},{10,34},{12,36},{14,38},{16,40}... | collective-permute-start | bytes 49160 | tf_op jit(solution)/shard_map/ppermute | solution.py:17
  164.8 5.0 %collective-permute-done.4 = bf16[64,128]{1,0:T(8,128)(2,1)S(1)} collective-permute-done((bf16[64,128]{1,0:T(8,128)(2,1)S(1)}, bf16[64,128]{1,0:T(8,128)(2,1)S(1)}, u32[]{:S(2)}, u32[]{:S(2)}) %collective-permute-start.4) | collective-permute-done | bytes 16416 | tf_op jit(solution)/shard_map/ppermute | solution.py:17
  169.9 3.6 %collective-permute-done.9 = bf16[64,128]{1,0:T(8,128)(2,1)S(1)} collective-permute-done((bf16[64,128]{1,0:T(8,128)(2,1)S(1)}, bf16[64,128]{1,0:T(8,128)(2,1)S(1)}, u32[]{:S(2)}, u32[]{:S(2)}) %collective-permute-start.9) | collective-permute-done | bytes 16416 | tf_op jit(solution)/shard_map/ppermute | solution.py:17
  173.5 2.5 %collective-permute-start.12 = (bf16[8,64,128]{2,1,0:T(8,128)(2,1)S(1)}, bf16[8,64,128]{2,1,0:T(8,128)(2,1)S(1)}, u32[]{:S(2)}, u32[]{:S(2)}) collective-permute-start(bf16[8,64,128]{2,1,0:T(8,128)(2,1)S(1)} %constant_dynamic-update-slice_fusion), channel_id=1, source_target_pairs={{0,6},{2,0},{4,2},{6,4},{8,14},{10,8},{12,10},{14,12},{16,22},{18,... | collective-permute-start | bytes 393224 | tf_op jit(solution)/shard_map/ppermute | solution.py:17
  178.7 3.9 %collective-permute-done.11 = bf16[8,64,128]{2,1,0:T(8,128)(2,1)S(1)} collective-permute-done((bf16[8,64,128]{2,1,0:T(8,128)(2,1)S(1)}, bf16[8,64,128]{2,1,0:T(8,128)(2,1)S(1)}, u32[]{:S(2)}, u32[]{:S(2)}) %collective-permute-start.11) | collective-permute-done | bytes 131104 | tf_op jit(solution)/shard_map/ppermute | solution.py:17
  185.8 2.8 %collective-permute-start.15 = (bf16[4,8,64,128]{3,2,1,0:T(8,128)(2,1)S(1)}, bf16[4,8,64,128]{3,2,1,0:T(8,128)(2,1)S(1)}, u32[]{:S(2)}, u32[]{:S(2)}) collective-permute-start(bf16[4,8,64,128]{3,2,1,0:T(8,128)(2,1)S(1)} %get-tuple-element.14), channel_id=1, source_target_pairs={{0,192},{2,194},{4,196},{6,198},{8,200},{10,202},{12,204},{14,206}... | collective-permute-start | bytes 1572872 | tf_op jit(solution)/shard_map/ppermute | solution.py:17
  188.6 11.5 %collective-permute-done.14 = bf16[4,8,64,128]{3,2,1,0:T(8,128)(2,1)S(1)} collective-permute-done((bf16[4,8,64,128]{3,2,1,0:T(8,128)(2,1)S(1)}, bf16[4,8,64,128]{3,2,1,0:T(8,128)(2,1)S(1)}, u32[]{:S(2)}, u32[]{:S(2)}) %collective-permute-start.14) | collective-permute-done | bytes 524320 | tf_op jit(solution)/shard_map/ppermute | solution.py:17
  200.1 5.6 %collective-permute-done.13 = bf16[4,8,64,128]{3,2,1,0:T(8,128)(2,1)S(1)} collective-permute-done((bf16[4,8,64,128]{3,2,1,0:T(8,128)(2,1)S(1)}, bf16[4,8,64,128]{3,2,1,0:T(8,128)(2,1)S(1)}, u32[]{:S(2)}, u32[]{:S(2)}) %collective-permute-start.13) | collective-permute-done | bytes 524320 | tf_op jit(solution)/shard_map/ppermute | solution.py:17
  206.0 1.8 fusion.32
  209.2 8.6 %subtract_convert_fusion = bf16[128,64,128]{2,1,0:T(8,128)(2,1)} fusion(f32[128,64,128]{2,1,0:T(8,128)} %get-tuple-element.8, f32[128,64,128]{2,1,0:T(8,128)S(1)} %copy-done.2, bf16[128,128,128]{2,0,1:T(8,128)(2,1)S(1)} %copy-done.1, bf16[128,64,128]{2,0,1:T(8,128)(2,1)S(1)} %fusion.32), kind=kOutput, calls=%fused_computation.16 | convolution fusion | flops 271581184 | bytes 16777216 | tf_op jit(solution)/shard_map/pca,pba->pcb/dot_general | solution.py:100
  (56 shorter events, 15.0 us)
Async XLA Ops:
  6.5 6.1 %copy-start = (bf16[8,128,128]{2,1,0:T(8,128)(2,1)S(1)}, bf16[8,128,128]{2,1,0:T(8,128)(2,1)}, u32[]{:S(2)}) copy-start(bf16[8,128,128]{2,1,0:T(8,128)(2,1)} %param.10) | copy-start | bytes 786436
  6.5 10.0 %copy-start.5 = (f32[128,128]{1,0:T(8,128)S(1)}, f32[128,128]{1,0:T(8,128)}, u32[]{:S(2)}) copy-start(f32[128,128]{1,0:T(8,128)} %param.13) | copy-start | bytes 196612
  6.5 10.0 %copy-start.3 = (bf16[128,64,128]{2,1,0:T(8,128)(2,1)S(1)}, bf16[128,64,128]{2,1,0:T(8,128)(2,1)}, u32[]{:S(2)}) copy-start(bf16[128,64,128]{2,1,0:T(8,128)(2,1)} %param.9) | copy-start | bytes 6291460
  6.5 136.5 %all-gather.3.cloned.1.call-start = ((), (), s32[]{:S(2)}) async-start(), calls=%async_computation.1 | async-start | bytes 8454144 | tf_op jit(solution)/shard_map/all_gather | solution.py:34
  7.3 14.0 %collective-permute-start = (bf16[128,64,128]{2,1,0:T(8,128)(2,1)}, bf16[128,64,128]{2,1,0:T(8,128)(2,1)}, u32[]{:S(2)}, u32[]{:S(2)}) collective-permute-start(bf16[128,64,128]{2,1,0:T(8,128)(2,1)} %param.8), channel_id=1, source_target_pairs={{0,1},{1,0},{2,3},{3,2},{4,5},{5,4},{6,7},{7,6},{8,9},{9,8},{10,11... | collective-permute-start | bytes 6291464 | tf_op jit(solution)/shard_map/ppermute | solution.py:37
  10.9 5.7 %copy-start.4 = (bf16[128,64,128]{2,1,0:T(8,128)(2,1)S(1)}, bf16[128,64,128]{2,1,0:T(8,128)(2,1)}, u32[]{:S(2)}) copy-start(bf16[128,64,128]{2,1,0:T(8,128)(2,1)} %param.8) | copy-start | bytes 6291460
  115.4 4.3 %collective-permute-start.1 = (bf16[128,64,128]{2,1,0:T(8,128)(2,1)S(1)}, bf16[128,64,128]{2,1,0:T(8,128)(2,1)}, u32[]{:S(2)}, u32[]{:S(2)}) collective-permute-start(bf16[128,64,128]{2,1,0:T(8,128)(2,1)S(1)} %all_to_all.5), channel_id=1, source_target_pairs={{0,1},{1,0},{2,3},{3,2},{4,5},{5,4},{6,7},{7,6},{8,9},{9,8},{10,11... | collective-permute-start | bytes 6291464 | tf_op jit(solution)/shard_map/ppermute | solution.py:70
  143.0 7.6 %copy-start.6 = (bf16[1,256,128]{2,1,0:T(8,128)(2,1)S(1)}, bf16[1,256,128]{2,1,0:T(8,128)(2,1)}, u32[]{:S(2)}) copy-start(bf16[1,256,128]{2,1,0:T(8,128)(2,1)} %param.12) | copy-start | bytes 196612
  150.8 1.3 collective-permute-start.2
  152.1 11.9 %collective-permute-start.3 = (bf16[64,128]{1,0:T(8,128)(2,1)S(1)}, bf16[64,128]{1,0:T(8,128)(2,1)S(1)}, u32[]{:S(2)}, u32[]{:S(2)}) collective-permute-start(bf16[64,128]{1,0:T(8,128)(2,1)S(1)} %get-tuple-element.12), channel_id=1, source_target_pairs={{0,8},{2,10},{4,12},{6,14},{8,16},{10,18},{12,20},{14,22},{16,24},... | collective-permute-start | bytes 49160 | tf_op jit(solution)/shard_map/ppermute | solution.py:17
  153.4 16.4 %collective-permute-start.8 = (bf16[64,128]{1,0:T(8,128)(2,1)S(1)}, bf16[64,128]{1,0:T(8,128)(2,1)S(1)}, u32[]{:S(2)}, u32[]{:S(2)}) collective-permute-start(bf16[64,128]{1,0:T(8,128)(2,1)S(1)} %get-tuple-element.12), channel_id=1, source_target_pairs={{0,48},{2,50},{4,52},{6,54},{8,56},{10,58},{12,60},{14,62},{16,0},... | collective-permute-start | bytes 49160 | tf_op jit(solution)/shard_map/ppermute | solution.py:17
  156.4 13.4 %collective-permute-start.7 = (bf16[64,128]{1,0:T(8,128)(2,1)S(1)}, bf16[64,128]{1,0:T(8,128)(2,1)S(1)}, u32[]{:S(2)}, u32[]{:S(2)}) collective-permute-start(bf16[64,128]{1,0:T(8,128)(2,1)S(1)} %get-tuple-element.12), channel_id=1, source_target_pairs={{0,40},{2,42},{4,44},{6,46},{8,48},{10,50},{12,52},{14,54},{16,56}... | collective-permute-start | bytes 49160 | tf_op jit(solution)/shard_map/ppermute | solution.py:17
  157.0 12.9 %collective-permute-start.6 = (bf16[64,128]{1,0:T(8,128)(2,1)S(1)}, bf16[64,128]{1,0:T(8,128)(2,1)S(1)}, u32[]{:S(2)}, u32[]{:S(2)}) collective-permute-start(bf16[64,128]{1,0:T(8,128)(2,1)S(1)} %get-tuple-element.12), channel_id=1, source_target_pairs={{0,32},{2,34},{4,36},{6,38},{8,40},{10,42},{12,44},{14,46},{16,48}... | collective-permute-start | bytes 49160 | tf_op jit(solution)/shard_map/ppermute | solution.py:17
  160.1 9.7 %collective-permute-start.5 = (bf16[64,128]{1,0:T(8,128)(2,1)S(1)}, bf16[64,128]{1,0:T(8,128)(2,1)S(1)}, u32[]{:S(2)}, u32[]{:S(2)}) collective-permute-start(bf16[64,128]{1,0:T(8,128)(2,1)S(1)} %get-tuple-element.12), channel_id=1, source_target_pairs={{0,24},{2,26},{4,28},{6,30},{8,32},{10,34},{12,36},{14,38},{16,40}... | collective-permute-start | bytes 49160 | tf_op jit(solution)/shard_map/ppermute | solution.py:17
  163.9 5.8 %collective-permute-start.4 = (bf16[64,128]{1,0:T(8,128)(2,1)S(1)}, bf16[64,128]{1,0:T(8,128)(2,1)S(1)}, u32[]{:S(2)}, u32[]{:S(2)}) collective-permute-start(bf16[64,128]{1,0:T(8,128)(2,1)S(1)} %get-tuple-element.12), channel_id=1, source_target_pairs={{0,16},{2,18},{4,20},{6,22},{8,24},{10,26},{12,28},{14,30},{16,32}... | collective-permute-start | bytes 49160 | tf_op jit(solution)/shard_map/ppermute | solution.py:17
  169.8 3.7 %collective-permute-start.9 = (bf16[64,128]{1,0:T(8,128)(2,1)S(1)}, bf16[64,128]{1,0:T(8,128)(2,1)S(1)}, u32[]{:S(2)}, u32[]{:S(2)}) collective-permute-start(bf16[64,128]{1,0:T(8,128)(2,1)S(1)} %get-tuple-element.12), channel_id=1, source_target_pairs={{0,56},{2,58},{4,60},{6,62},{8,0},{10,2},{12,4},{14,6},{16,8},{18,... | collective-permute-start | bytes 49160 | tf_op jit(solution)/shard_map/ppermute | solution.py:17
  173.5 5.1 %collective-permute-start.12 = (bf16[8,64,128]{2,1,0:T(8,128)(2,1)S(1)}, bf16[8,64,128]{2,1,0:T(8,128)(2,1)S(1)}, u32[]{:S(2)}, u32[]{:S(2)}) collective-permute-start(bf16[8,64,128]{2,1,0:T(8,128)(2,1)S(1)} %constant_dynamic-update-slice_fusion), channel_id=1, source_target_pairs={{0,6},{2,0},{4,2},{6,4},{8,14},{10,8},{12,10},{14,12},{16,22},{18,... | collective-permute-start | bytes 393224 | tf_op jit(solution)/shard_map/ppermute | solution.py:17
  176.0 6.5 %collective-permute-start.11 = (bf16[8,64,128]{2,1,0:T(8,128)(2,1)S(1)}, bf16[8,64,128]{2,1,0:T(8,128)(2,1)S(1)}, u32[]{:S(2)}, u32[]{:S(2)}) collective-permute-start(bf16[8,64,128]{2,1,0:T(8,128)(2,1)S(1)} %constant_dynamic-update-slice_fusion), channel_id=1, source_target_pairs={{0,4},{2,6},{4,0},{6,2},{8,12},{10,14},{12,8},{14,10},{16,20},{18,... | collective-permute-start | bytes 393224 | tf_op jit(solution)/shard_map/ppermute | solution.py:17
  177.1 6.9 %collective-permute-start.10 = (bf16[8,64,128]{2,1,0:T(8,128)(2,1)S(1)}, bf16[8,64,128]{2,1,0:T(8,128)(2,1)S(1)}, u32[]{:S(2)}, u32[]{:S(2)}) collective-permute-start(bf16[8,64,128]{2,1,0:T(8,128)(2,1)S(1)} %constant_dynamic-update-slice_fusion), channel_id=1, source_target_pairs={{0,2},{2,4},{4,6},{6,0},{8,10},{10,12},{12,14},{14,8},{16,18},{18,... | collective-permute-start | bytes 393224 | tf_op jit(solution)/shard_map/ppermute | solution.py:17
  184.0 16.1 %collective-permute-start.14 = (bf16[4,8,64,128]{3,2,1,0:T(8,128)(2,1)S(1)}, bf16[4,8,64,128]{3,2,1,0:T(8,128)(2,1)S(1)}, u32[]{:S(2)}, u32[]{:S(2)}) collective-permute-start(bf16[4,8,64,128]{3,2,1,0:T(8,128)(2,1)S(1)} %get-tuple-element.14), channel_id=1, source_target_pairs={{0,128},{2,130},{4,132},{6,134},{8,136},{10,138},{12,140},{14,142}... | collective-permute-start | bytes 1572872 | tf_op jit(solution)/shard_map/ppermute | solution.py:17
  185.4 20.3 %collective-permute-start.13 = (bf16[4,8,64,128]{3,2,1,0:T(8,128)(2,1)S(1)}, bf16[4,8,64,128]{3,2,1,0:T(8,128)(2,1)S(1)}, u32[]{:S(2)}, u32[]{:S(2)}) collective-permute-start(bf16[4,8,64,128]{3,2,1,0:T(8,128)(2,1)S(1)} %get-tuple-element.14), channel_id=1, source_target_pairs={{0,64},{2,66},{4,68},{6,70},{8,72},{10,74},{12,76},{14,78},{16,80}... | collective-permute-start | bytes 1572872 | tf_op jit(solution)/shard_map/ppermute | solution.py:17
  185.8 19.9 %collective-permute-start.15 = (bf16[4,8,64,128]{3,2,1,0:T(8,128)(2,1)S(1)}, bf16[4,8,64,128]{3,2,1,0:T(8,128)(2,1)S(1)}, u32[]{:S(2)}, u32[]{:S(2)}) collective-permute-start(bf16[4,8,64,128]{3,2,1,0:T(8,128)(2,1)S(1)} %get-tuple-element.14), channel_id=1, source_target_pairs={{0,192},{2,194},{4,196},{6,198},{8,200},{10,202},{12,204},{14,206}... | collective-permute-start | bytes 1572872 | tf_op jit(solution)/shard_map/ppermute | solution.py:17
  205.7 2.2 copy-start.1
  205.7 3.5 %copy-start.2 = (f32[128,64,128]{2,1,0:T(8,128)S(1)}, f32[128,64,128]{2,1,0:T(8,128)}, u32[]{:S(2)}) copy-start(f32[128,64,128]{2,1,0:T(8,128)} %get-tuple-element.10) | copy-start | bytes 12582916
  (1 other events, 1.8 us)
Sparse Core Ops, SparseCore 0:
  10.8 132.1 all-gather.2
